TPU v7x, 256 devices: a whole 4x4x8 slice. The times are simulated.
256 devices in a mesh: dp: 32 (over x, z), tensor: 8 (over y, core).
Axes of the slice: x: 4, y: 4, z: 8, core: 2. Of those that a mesh axis runs over, the one named last changes fastest.
Arguments:
- counts: int32 [32], replicated, may hold values from 1 to 32, 512 in all
- keys: bfloat16 [1024, 28672], P('dp'), may hold values from -6 to 6
- inverse_cov: bfloat16 [28672, 28672], P('tensor', 'dp'), as said below
- hidden: bfloat16 [1024, 8192], P('dp', 'tensor'), may hold values from -6 to 6
- targets: bfloat16 [1024, 8192], P('dp', 'tensor'), may hold values from -48 to 48
- down_weight: bfloat16 [8192, 28672], P('tensor', 'dp'), may hold values from -0.03125 to 0.03125
Outputs:
- new_weight: bfloat16 [8192, 28672], P('tensor', 'dp')
- next_resid: bfloat16 [1024, 8192], P('dp', 'tensor')
Inputs may be any that keep to these rules, and one draw needn't show every extreme that they name: Group g has counts[g] live edits in its first counts[g] slots; the counts sum to 512; some group holds 32. `inverse_cov`: symmetric positive definite.
All inputs are finite; a program needn't handle non-finite values.
Results may differ from a plain program's by a relative error of at most 0.01.
The roundings to bfloat16 on the way count: a program that leaves them out, or rounds other values in their place, can miss the bound.
Values may be sent and summed in bfloat16 or wider, within the bound.
No kernel may reach another device: no remote copies, remote signals or barrier semaphores. Data moves between devices by JAX's collectives and lax.ppermute only.
A program may use at most 128 MiB of HBM per device.

v0:
```python
import jax
import jax.numpy as jnp
from jax import lax
from jax.sharding import PartitionSpec as P

LAYERS_LEFT = 3


def cholesky_solve(system, right_side):
    factor = jnp.linalg.cholesky(system)
    middle = lax.linalg.triangular_solve(factor, right_side, left_side=True, lower=True)
    return lax.linalg.triangular_solve(factor, middle, left_side=True, lower=True, transpose_a=True)


def rows_product(left, right):
    return lax.dot_general(
        left, right, (((1,), (1,)), ((), ())), preferred_element_type=jnp.float32
    )


def per_device(counts, keys, inverse_cov, hidden, targets, down_weight):
    slot_count = keys.shape[0]
    group_size = lax.axis_size("dp")
    group_index = lax.axis_index("dp")
    tensor_index = lax.axis_index("tensor")
    width_part = inverse_cov.shape[0]
    live_slot = (jnp.arange(slot_count, dtype=jnp.int32) < counts[group_index])[:, None]
    masked_keys = jnp.where(live_slot, keys, jnp.zeros_like(keys))
    column_part = lax.dynamic_slice_in_dim(masked_keys, tensor_index * width_part, width_part, 1)
    columns = lax.all_to_all(masked_keys, "dp", split_axis=1, concat_axis=0, tiled=True)
    partial_q = jnp.dot(
        lax.all_gather(column_part, "dp", axis=0, tiled=True),
        inverse_cov,
        preferred_element_type=jnp.float32,
    )
    row_total = slot_count * group_size
    precond = lax.psum(partial_q, "tensor").astype(jnp.bfloat16)
    gram_matrix = lax.psum(rows_product(precond, columns), "dp")
    system = gram_matrix + jnp.eye(row_total, dtype=jnp.float32)
    change = (targets.astype(jnp.float32) - hidden.astype(jnp.float32)) / LAYERS_LEFT
    resid_local = jnp.where(live_slot, change, jnp.zeros_like(change)).astype(jnp.bfloat16)
    resid_all = lax.all_gather(resid_local, "dp", axis=0, tiled=True)
    solved = cholesky_solve(system, resid_all.astype(jnp.float32)).astype(jnp.bfloat16)
    weight_delta = lax.dot_general(
        solved, precond, (((0,), (0,)), ((), ())), preferred_element_type=jnp.float32
    )
    new_weight = (down_weight.astype(jnp.float32) + weight_delta).astype(jnp.bfloat16)
    recomputed = lax.psum_scatter(
        rows_product(columns, new_weight), "dp", scatter_dimension=0, tiled=True
    )
    summed = hidden.astype(jnp.float32) + recomputed
    next_resid = jnp.where(live_slot, summed, jnp.zeros_like(summed)).astype(jnp.bfloat16)
    return (new_weight, next_resid)


def solution(mesh):
    in_specs = (
        P(),
        P("dp", None),
        P("tensor", "dp"),
        P("dp", "tensor"),
        P("dp", "tensor"),
        P("tensor", "dp"),
    )
    out_specs = (P("tensor", "dp"), P("dp", "tensor"))
    return jax.shard_map(
        per_device, mesh=mesh, in_specs=in_specs, out_specs=out_specs, check_vma=False
    )
```

profile of v0, /device:TPU:2, one launch (start us, length us, event | category | flops | bytes accessed | tf_op | source)
XLA Modules:
  0.0 960.3 jit_solution(10963349034254447557)
XLA Ops:
  13.0 11.6 %all-to-all-start = ((bf16[32,32,896]{2,0,1:T(8,128)(2,1)}), bf16[32,32,896]{2,0,1:T(8,128)(2,1)S(1)}, u32[]{:S(2)}, u32[]{:S(2)}) async-start(bf16[32,32,896]{2,0,1:T(8,128)(2,1)} %bitcast.144), calls=%async_computation | async-start | bytes 3670016 | tf_op jit(solution)/shard_map/all_to_all | solution.py:30
  25.4 91.7 %all-gather.3.cloned.1.call-done = bf16[1024,3584]{1,0:T(8,128)(2,1)} async-done(((bf16[32,3584]{1,0:T(8,128)(2,1)}), bf16[1024,3584]{1,0:T(8,128)(2,1)}) %all-gather.3.cloned.1.call-update) | async-done | bytes 7340048 | tf_op jit(solution)/shard_map/all_gather | solution.py:32
  117.2 13.1 %fusion.120 = f32[1024,896]{1,0:T(8,128)} fusion(bf16[1024,3584]{1,0:T(8,128)(2,1)} %all-gather.3.cloned.1.call-done, bf16[3584,896]{1,0:T(8,128)(2,1)} %param.8), kind=kOutput, calls=%fused_computation.235 | convolution fusion | flops 6576668672 | bytes 17432576 | tf_op jit(solution)/shard_map/dot_general | solution.py:31
  130.3 57.6 %all-reduce.5 = bf16[1024,896]{1,0:T(8,128)(2,1)} all-reduce(f32[1024,896]{1,0:T(8,128)} %fusion.120), channel_id=1, replica_groups=mesh['dp'=32,'tensor'=8] {'tensor'}, use_global_device_ids=true, to_apply=%region_0.1 | all-reduce | flops 917504 | bytes 5505024 | tf_op jit(solution)/shard_map/psum | solution.py:37
  187.9 5.8 fusion.122
  195.6 4.0 convert_element_type.35
  199.6 160.8 %all-reduce.4.cloned.1.call-done = f32[1024,1024]{0,1:T(8,128)} async-done(((f32[1024,1024]{0,1:T(8,128)}), f32[1024,1024]{0,1:T(8,128)}) %all-reduce.4.cloned.1.call-update) | async-done | bytes 4194320 | tf_op jit(solution)/shard_map/psum | solution.py:38
  360.4 4.8 convert_add_fusion
  365.2 5.5 copy.17
  370.7 4.5 fusion
  377.2 11.7 %cholesky.223 = f32[128,128]{1,0:T(8,128)S(1)} custom-call(f32[128,128]{1,0:T(8,128)S(1)} %cholesky.580), custom_call_target="Cholesky" | custom-call | tf_op jit(solution)/shard_map/jit(cholesky)/cholesky | solution.py:10
  388.9 9.8 %custom-call.64 = f32[1,128,128]{1,2,0:T(8,128)S(1)} custom-call(f32[1,128,128]{2,1,0:T(8,128)S(1)} %get-tuple-element.58), custom_call_target="InvertDiagBlocksLowerTriangular" | custom-call | tf_op jit(solution)/shard_map/jit(cholesky)/cholesky | solution.py:10
  398.7 2.5 cholesky.255
  405.1 12.1 %cholesky.244 = f32[128,128]{1,0:T(8,128)S(1)} custom-call(f32[128,128]{1,0:T(8,128)S(1)} %cholesky.584), custom_call_target="Cholesky" | custom-call | tf_op jit(solution)/shard_map/jit(cholesky)/cholesky | solution.py:10
  417.9 9.8 %custom-call.65 = f32[1,128,128]{1,2,0:T(8,128)S(1)} custom-call(f32[1,128,128]{2,1,0:T(8,128)S(1)} %get-tuple-element.55), custom_call_target="InvertDiagBlocksLowerTriangular" | custom-call | tf_op jit(solution)/shard_map/jit(cholesky)/cholesky | solution.py:10
  431.1 11.7 %cholesky.468 = f32[128,128]{1,0:T(8,128)S(1)} custom-call(f32[128,128]{1,0:T(8,128)S(1)} %cholesky.589), custom_call_target="Cholesky" | custom-call | tf_op jit(solution)/shard_map/jit(cholesky)/cholesky | solution.py:10
  444.1 9.8 %custom-call.66 = f32[1,128,128]{1,2,0:T(8,128)S(1)} custom-call(f32[1,128,128]{2,1,0:T(8,128)S(1)} %get-tuple-element.52), custom_call_target="InvertDiagBlocksLowerTriangular" | custom-call | tf_op jit(solution)/shard_map/jit(cholesky)/cholesky | solution.py:10
  457.4 11.9 %cholesky.487 = f32[128,128]{1,0:T(8,128)S(1)} custom-call(f32[128,128]{1,0:T(8,128)S(1)} %cholesky.594), custom_call_target="Cholesky" | custom-call | tf_op jit(solution)/shard_map/jit(cholesky)/cholesky | solution.py:10
  470.6 9.8 %custom-call.67 = f32[1,128,128]{1,2,0:T(8,128)S(1)} custom-call(f32[1,128,128]{2,1,0:T(8,128)S(1)} %get-tuple-element.49), custom_call_target="InvertDiagBlocksLowerTriangular" | custom-call | tf_op jit(solution)/shard_map/jit(cholesky)/cholesky | solution.py:10
  483.9 11.7 %cholesky.506 = f32[128,128]{1,0:T(8,128)S(1)} custom-call(f32[128,128]{1,0:T(8,128)S(1)} %cholesky.599), custom_call_target="Cholesky" | custom-call | tf_op jit(solution)/shard_map/jit(cholesky)/cholesky | solution.py:10
  497.0 10.0 %custom-call.68 = f32[1,128,128]{1,2,0:T(8,128)S(1)} custom-call(f32[1,128,128]{2,1,0:T(8,128)S(1)} %get-tuple-element.46), custom_call_target="InvertDiagBlocksLowerTriangular" | custom-call | tf_op jit(solution)/shard_map/jit(cholesky)/cholesky | solution.py:10
  510.3 11.7 %cholesky.526 = f32[128,128]{1,0:T(8,128)S(1)} custom-call(f32[128,128]{1,0:T(8,128)S(1)} %cholesky.604), custom_call_target="Cholesky" | custom-call | tf_op jit(solution)/shard_map/jit(cholesky)/cholesky | solution.py:10
  523.4 9.8 %custom-call.69 = f32[1,128,128]{1,2,0:T(8,128)S(1)} custom-call(f32[1,128,128]{2,1,0:T(8,128)S(1)} %get-tuple-element.43), custom_call_target="InvertDiagBlocksLowerTriangular" | custom-call | tf_op jit(solution)/shard_map/jit(cholesky)/cholesky | solution.py:10
  536.2 12.1 %cholesky.546 = f32[128,128]{1,0:T(8,128)S(1)} custom-call(f32[128,128]{1,0:T(8,128)S(1)} %cholesky.609), custom_call_target="Cholesky" | custom-call | tf_op jit(solution)/shard_map/jit(cholesky)/cholesky | solution.py:10
  549.6 9.8 %custom-call.70 = f32[1,128,128]{1,2,0:T(8,128)S(1)} custom-call(f32[1,128,128]{2,1,0:T(8,128)S(1)} %get-tuple-element.40), custom_call_target="InvertDiagBlocksLowerTriangular" | custom-call | tf_op jit(solution)/shard_map/jit(cholesky)/cholesky | solution.py:10
  562.1 11.7 %cholesky.564 = f32[128,128]{1,0:T(8,128)S(1)} custom-call(f32[128,128]{1,0:T(8,128)S(1)} %convolution_subtract_fusion.16), custom_call_target="Cholesky" | custom-call | tf_op jit(solution)/shard_map/jit(cholesky)/cholesky | solution.py:10
  580.7 4.8 select_select_fusion
  585.6 22.6 %while.1 = (s32[]{:T(128)}, f32[1024,1024]{1,0:T(8,128)}, s32[8,2]{0,1:T(2,128)S(1)}, f32[8,128,128]{2,1,0:T(8,128)S(1)}, s32[]{:T(128)}) while((s32[]{:T(128)}, f32[1024,1024]{1,0:T(8,128)}, s32[8,2]{0,1:T(2,128)S(1)}, f32[8,128,128]{2,1,0:T(8,128)S(1)}, s32[]{:T(128)}) %tuple.61), condition=%wide.while_cond, body=%wide.while_body.sunk | while | flops 2 | bytes 131189 | solution.py:12
  608.2 78.8 %custom-call.71 = f32[8,128,128]{1,2,0:T(8,128)S(1)} custom-call(f32[8,128,128]{2,1,0:T(8,128)S(1)} %get-tuple-element.9), custom_call_target="InvertDiagBlocksLowerTriangular" | custom-call | tf_op jit(solution)/shard_map/triangular_solve | solution.py:12
  722.5 2.5 add_convert_fusion
  726.2 4.3 fusion.121
  730.5 221.2 %reduce-scatter.2.cloned.1.call-done = f32[32,1024]{1,0:T(8,128)} async-done(((f32[1024,1024]{1,0:T(8,128)}), f32[32,1024]{1,0:T(8,128)}) %reduce-scatter.2.cloned.1.call-update) | async-done | bytes 131088 | tf_op jit(solution)/shard_map/reduce_scatter | solution.py:48
  (148 shorter events, 103.1 us)
Async XLA Ops:
  7.2 110.0 %all-gather.3.cloned.1.call-start = ((), (), s32[]{:S(2)}) async-start(), calls=%async_computation.2 | async-start | bytes 7569408 | tf_op jit(solution)/shard_map/all_gather | solution.py:32
  11.5 13.1 %copy-start.4 = (bf16[32,1024]{1,0:T(8,128)(2,1)S(1)}, bf16[32,1024]{1,0:T(8,128)(2,1)}, u32[]{:S(2)}) copy-start(bf16[32,1024]{1,0:T(8,128)(2,1)} %param.9) | copy-start | bytes 196612
  11.6 13.1 %copy-start.5 = (bf16[32,1024]{1,0:T(8,128)(2,1)S(1)}, bf16[32,1024]{1,0:T(8,128)(2,1)}, u32[]{:S(2)}) copy-start(bf16[32,1024]{1,0:T(8,128)(2,1)} %param.10) | copy-start | bytes 196612
  13.0 174.9 %all-to-all-start = ((bf16[32,32,896]{2,0,1:T(8,128)(2,1)}), bf16[32,32,896]{2,0,1:T(8,128)(2,1)S(1)}, u32[]{:S(2)}, u32[]{:S(2)}) async-start(bf16[32,32,896]{2,0,1:T(8,128)(2,1)} %bitcast.144), calls=%async_computation | async-start | bytes 3670016 | tf_op jit(solution)/shard_map/all_to_all | solution.py:30
  24.6 171.0 %all-gather.5.cloned.1.call-start = ((), (), s32[]{:S(2)}) async-start(), calls=%async_computation.4 | async-start | bytes 2162688 | tf_op jit(solution)/shard_map/all_gather | solution.py:42
  25.4 335.0 %all-reduce.4.cloned.1.call-start = ((), (), s32[]{:S(2)}) async-start(), calls=%async_computation.3 | async-start | bytes 8388608 | tf_op jit(solution)/shard_map/psum | solution.py:38
  193.8 758.0 %reduce-scatter.2.cloned.1.call-start = ((), (), s32[]{:S(2)}) async-start(), calls=%async_computation.5 | async-start | bytes 4325376 | tf_op jit(solution)/shard_map/reduce_scatter | solution.py:48
  375.2 2.0 copy-start.2
  686.9 4.0 copy-start
  690.2 3.6 copy-start.1
  720.4 1.5 copy-start.3
  720.4 2.0 copy-start.6
  725.0 1.2 copy-start.7
Sparse Core Ops, SparseCore 0:
  11.7 105.4 all-gather.2
  120.4 75.1 all-gather.4
  199.2 161.1 all-reduce.3
  730.6 221.0 reduce-scatter.1
where the time goes:
time: 967 us; the launch traced here: 960 us
  waiting for transfers between devices  476 us (49%)
  other arithmetic  274 us (28%)
  matrix products  81.8 us (8%)
  blocking collectives  57.6 us (6%)
  local copies, waits for them, and re-layouts  38.9 us (4%)
  between operations  20 us (2%)
  starting transfers between devices  11.8 us (1%)
    reduce_scatter x1, waiting for transfers between devices, per_device(): lax.psum_scatter(rows_product(columns, new_weight), 'dp', scatter_dimensi...  221 us
    another operation x30, other arithmetic, cholesky_solve(): factor = jnp.linalg.cholesky(system)  173 us
    psum x1, waiting for transfers between devices, per_device(): gram_matrix = lax.psum(rows_product(precond, columns), 'dp')  161 us
    all_gather x1, waiting for transfers between devices, per_device(): lax.all_gather(column_part, 'dp', axis=0, tiled=True)  91.7 us
    another operation x4, other arithmetic, cholesky_solve(): lax.linalg.triangular_solve(factor, middle, left_side=True, lower=True, t...  83.6 us
    psum x1, blocking collectives, per_device(): precond = lax.psum(partial_q, 'tensor').astype(jnp.bfloat16)  57.6 us
    another operation x14, matrix products, cholesky_solve(): factor = jnp.linalg.cholesky(system)  23.1 us
    another operation x24, local copies, waits for them, and re-layouts  22.4 us
  transfers between devices with their start and end apart: 5, of which 4 were waited for; matrix products, arithmetic and copies ran while one was open for 3% of the time, Pallas kernels for 0%

commit v1 on v0

v1 whole, which is shorter than its diff:
```python
import jax
import jax.numpy as jnp
from jax import lax
from jax.sharding import PartitionSpec as P

LAYERS_LEFT = 3


def cholesky_solve(system, right_side):
    factor = jnp.linalg.cholesky(system)
    middle = lax.linalg.triangular_solve(factor, right_side, left_side=True, lower=True)
    return lax.linalg.triangular_solve(factor, middle, left_side=True, lower=True, transpose_a=True)


def rows_product(left, right):
    return lax.dot_general(
        left, right, (((1,), (1,)), ((), ())), preferred_element_type=jnp.float32
    )


def pick(select, values):
    return jnp.dot(select, values, preferred_element_type=jnp.float32).astype(values.dtype)


def per_device(counts, keys, inverse_cov, hidden, targets, down_weight):
    slot_count = keys.shape[0]
    group_size = lax.axis_size("dp")
    group_index = lax.axis_index("dp")
    tensor_index = lax.axis_index("tensor")
    width_part = inverse_cov.shape[0]
    row_total = slot_count * group_size
    live_total = row_total // 2

    ends = jnp.cumsum(counts)
    starts = ends - counts
    compact = jnp.arange(live_total, dtype=jnp.int32)
    owner = jnp.minimum(jnp.sum(compact[:, None] >= ends[None, :], axis=1), group_size - 1)
    row_of = owner * slot_count + compact - starts[owner]
    select = (row_of[:, None] == jnp.arange(row_total, dtype=jnp.int32)[None, :]).astype(jnp.bfloat16)

    slots = jnp.arange(slot_count, dtype=jnp.int32)
    live_vec = slots < counts[group_index]
    live_slot = live_vec[:, None]
    own_compact = jnp.where(live_vec, starts[group_index] + slots, 0)

    masked_keys = jnp.where(live_slot, keys, jnp.zeros_like(keys))
    column_part = lax.dynamic_slice_in_dim(masked_keys, tensor_index * width_part, width_part, 1)
    columns = lax.all_to_all(masked_keys, "dp", split_axis=1, concat_axis=0, tiled=True)
    gathered = lax.all_gather(column_part, "dp", axis=0, tiled=True)
    keys_c = pick(select, gathered)
    columns_c = pick(select, columns)
    partial_q = jnp.dot(keys_c, inverse_cov, preferred_element_type=jnp.float32)
    precond_c = lax.psum(partial_q, "tensor").astype(jnp.bfloat16)
    gram_c = lax.psum(rows_product(precond_c, columns_c), "dp")

    base_partial = rows_product(columns, down_weight)
    gram_c, base_partial = lax.optimization_barrier((gram_c, base_partial))
    base = lax.psum_scatter(base_partial, "dp", scatter_dimension=0, tiled=True)

    system = gram_c + jnp.eye(live_total, dtype=jnp.float32)
    change = (targets.astype(jnp.float32) - hidden.astype(jnp.float32)) / LAYERS_LEFT
    resid_local = jnp.where(live_slot, change, jnp.zeros_like(change)).astype(jnp.bfloat16)
    resid_all = lax.all_gather(resid_local, "dp", axis=0, tiled=True)
    resid_c = pick(select, resid_all)
    solved_c = cholesky_solve(system, resid_c.astype(jnp.float32)).astype(jnp.bfloat16)
    weight_delta = lax.dot_general(
        solved_c, precond_c, (((0,), (0,)), ((), ())), preferred_element_type=jnp.float32
    )
    new_weight = (down_weight.astype(jnp.float32) + weight_delta).astype(jnp.bfloat16)

    gram_own = jnp.where(live_slot, jnp.take(gram_c, own_compact, axis=1).T, 0.0)
    extra = jnp.dot(
        gram_own, solved_c.astype(jnp.float32),
        precision=lax.Precision.HIGHEST, preferred_element_type=jnp.float32,
    )
    summed = hidden.astype(jnp.float32) + (base + extra)
    next_resid = jnp.where(live_slot, summed, jnp.zeros_like(summed)).astype(jnp.bfloat16)
    return (new_weight, next_resid)


def solution(mesh):
    in_specs = (
        P(),
        P("dp", None),
        P("tensor", "dp"),
        P("dp", "tensor"),
        P("dp", "tensor"),
        P("tensor", "dp"),
    )
    out_specs = (P("tensor", "dp"), P("dp", "tensor"))
    return jax.shard_map(
        per_device, mesh=mesh, in_specs=in_specs, out_specs=out_specs, check_vma=False
    )
```

time: 967 us -> 589 us (0.61)
  waiting for transfers between devices: 476 us -> 286 us
  other arithmetic: 274 us -> 148 us
  matrix products: 81.8 us -> 45.4 us
  local copies, waits for them, and re-layouts: 38.9 us -> 17.8 us
    reduce_scatter x1, waiting for transfers between devices: 221 us -> 73.1 us  [per_device(): base = lax.psum_scatter(base_partial, 'dp', scatter_dimension=0, tiled=True)]
    another operation x30 -> x14, other arithmetic: 173 us -> 78.9 us  [cholesky_solve(): factor = jnp.linalg.cholesky(system)]
    another operation x4 -> x3, other arithmetic: 83.6 us -> 40.7 us  [cholesky_solve(): lax.linalg.triangular_solve(factor, middle, left_side=True, lower=True, t...]
    all_gather x1, waiting for transfers between devices: 91.7 us -> 67.5 us  [per_device(): gathered = lax.all_gather(column_part, 'dp', axis=0, tiled=True)]
    another operation x14 -> x6, matrix products: 23.1 us -> 1.87 us  [cholesky_solve(): factor = jnp.linalg.cholesky(system)]
    sub x0 -> x2, other arithmetic: none -> 15.7 us  [the longest x1 15.7 us: per_device(): row_of = owner * slot_count + compact - starts[owner]]
    psum x1, waiting for transfers between devices: 161 us -> 145 us  [per_device(): gram_c = lax.psum(rows_product(precond_c, columns_c), 'dp')]
    another operation x24 -> x13, local copies, waits for them, and re-layouts: 22.4 us -> 10.1 us
  transfers between devices with their start and end apart: 5 -> 5, of which waited for: 4 -> 3; matrix products, arithmetic and copies ran while one was open for 3% -> 35% of each run, Pallas kernels for 0% -> 0%
where the time goes in v1:
time: 589 us; the launch traced here: 581 us
  waiting for transfers between devices  286 us (49%)
  other arithmetic  148 us (25%)
  blocking collectives  54.6 us (9%)
  matrix products  45.4 us (8%)
  local copies, waits for them, and re-layouts  17.8 us (3%)
  between operations  16.9 us (3%)
  starting transfers between devices  12.1 us (2%)
    psum x1, waiting for transfers between devices, per_device(): gram_c = lax.psum(rows_product(precond_c, columns_c), 'dp')  145 us
    another operation x14, other arithmetic, cholesky_solve(): factor = jnp.linalg.cholesky(system)  78.9 us
    reduce_scatter x1, waiting for transfers between devices, per_device(): base = lax.psum_scatter(base_partial, 'dp', scatter_dimension=0, tiled=True)  73.1 us
    all_gather x1, waiting for transfers between devices, per_device(): gathered = lax.all_gather(column_part, 'dp', axis=0, tiled=True)  67.5 us
    psum x1, blocking collectives, per_device(): precond_c = lax.psum(partial_q, 'tensor').astype(jnp.bfloat16)  54.6 us
    another operation x3, other arithmetic, cholesky_solve(): lax.linalg.triangular_solve(factor, middle, left_side=True, lower=True, t...  40.7 us
    sub x1, other arithmetic, per_device(): row_of = owner * slot_count + compact - starts[owner]  15.7 us
    dot_general x1, matrix products, per_device(): partial_q = jnp.dot(keys_c, inverse_cov, preferred_element_type=jnp.float32)  14 us
  transfers between devices with their start and end apart: 5, of which 3 were waited for; matrix products, arithmetic and copies ran while one was open for 35% of the time, Pallas kernels for 0%

profile of v1, /device:TPU:2, one launch (start us, length us, event | category | flops | bytes accessed | tf_op | source)
XLA Modules:
  0.0 580.7 jit_solution(14730715012602335396)
XLA Ops:
  9.0 1.7 broadcast_select_fusion
  11.4 1.4 copy.29
  12.8 11.7 %all-to-all-start = ((bf16[32,32,896]{2,0,1:T(8,128)(2,1)}), bf16[32,32,896]{2,0,1:T(8,128)(2,1)S(1)}, u32[]{:S(2)}, u32[]{:S(2)}) async-start(bf16[32,32,896]{2,0,1:T(8,128)(2,1)} %bitcast.118), calls=%async_computation | async-start | bytes 3670016 | tf_op jit(solution)/shard_map/all_to_all | solution.py:48
  27.2 4.5 compare_select_fusion.1
  31.9 15.7 %select_subtract_fusion = s32[512]{0:T(512)S(1)} fusion(pred[512]{0:T(512)(128)(4,1)S(1)} %get-tuple-element.38, pred[512]{0:T(512)(128)(4,1)S(1)} %get-tuple-element.37, pred[512]{0:T(512)(128)(4,1)S(1)} %get-tuple-element.36, pred[512]{0:T(512)(128)(4,1)S(1)} %get-tuple-element.35, pred[512]{0:T(512)(128)(4,1)S(1)} %get-tuple-element.34, ...), kind=kLoop, calls=%fused_computation.145 | loop fusion | flops 14848 | bytes 19044 | tf_op jit(solution)/shard_map/sub | solution.py:38
  49.3 67.5 %all-gather.3.cloned.1.call-done = bf16[1024,3584]{1,0:T(8,128)(2,1)} async-done(((bf16[32,3584]{1,0:T(8,128)(2,1)}), bf16[1024,3584]{1,0:T(8,128)(2,1)}) %all-gather.3.cloned.1.call-update) | async-done | bytes 7340048 | tf_op jit(solution)/shard_map/all_gather | solution.py:49
  116.9 14.0 %fusion.35 = f32[512,896]{1,0:T(8,128)} fusion(bf16[3584,896]{1,0:T(8,128)(2,1)} %param.8, bf16[1024,3584]{1,0:T(8,128)(2,1)} %all-gather.3.cloned.1.call-done, s32[512]{0:T(512)S(1)} %select_subtract_fusion), kind=kOutput, calls=%fused_computation.56 | convolution fusion | flops 7048790016 | bytes 15599616 | tf_op jit(solution)/shard_map/dot_general | solution.py:52
  130.8 54.6 %all-reduce.5 = bf16[512,896]{1,0:T(8,128)(2,1)S(1)} all-reduce(f32[512,896]{1,0:T(8,128)} %fusion.35), channel_id=1, replica_groups=mesh['dp'=32,'tensor'=8] {'tensor'}, use_global_device_ids=true, to_apply=%region_2.3 | all-reduce | flops 458752 | bytes 2752512 | tf_op jit(solution)/shard_map/psum | solution.py:53
  185.5 2.8 fusion.36
  188.6 1.7 compare_and_fusion
  190.3 5.8 fusion.89
  196.1 4.5 fusion.85
  200.7 145.4 %all-reduce.4.cloned.1.call-done = f32[512,512]{0,1:T(8,128)} async-done(((f32[512,512]{0,1:T(8,128)}), f32[512,512]{0,1:T(8,128)}) %all-reduce.4.cloned.1.call-update) | async-done | bytes 1048592 | tf_op jit(solution)/shard_map/psum | solution.py:54
  346.1 1.3 convert_add_fusion
  349.3 11.7 %cholesky.104 = f32[128,128]{1,0:T(8,128)S(1)} custom-call(f32[128,128]{1,0:T(8,128)S(1)} %cholesky.266), custom_call_target="Cholesky" | custom-call | tf_op jit(solution)/shard_map/jit(cholesky)/cholesky | solution.py:10
  361.1 9.8 %custom-call.32 = f32[1,128,128]{1,2,0:T(8,128)S(1)} custom-call(f32[1,128,128]{2,1,0:T(8,128)S(1)} %get-tuple-element.60), custom_call_target="InvertDiagBlocksLowerTriangular" | custom-call | tf_op jit(solution)/shard_map/jit(cholesky)/cholesky | solution.py:10
  371.6 12.1 %cholesky.217 = f32[128,128]{1,0:T(8,128)S(1)} custom-call(f32[128,128]{1,0:T(8,128)S(1)} %cholesky.270), custom_call_target="Cholesky" | custom-call | tf_op jit(solution)/shard_map/jit(cholesky)/cholesky | solution.py:10
  383.8 9.8 %custom-call.33 = f32[1,128,128]{1,2,0:T(8,128)S(1)} custom-call(f32[1,128,128]{2,1,0:T(8,128)S(1)} %get-tuple-element.57), custom_call_target="InvertDiagBlocksLowerTriangular" | custom-call | tf_op jit(solution)/shard_map/jit(cholesky)/cholesky | solution.py:10
  394.2 11.7 %cholesky.238 = f32[128,128]{1,0:T(8,128)S(1)} custom-call(f32[128,128]{1,0:T(8,128)S(1)} %cholesky.275), custom_call_target="Cholesky" | custom-call | tf_op jit(solution)/shard_map/jit(cholesky)/cholesky | solution.py:10
  406.0 9.8 %custom-call.34 = f32[1,128,128]{1,2,0:T(8,128)S(1)} custom-call(f32[1,128,128]{2,1,0:T(8,128)S(1)} %get-tuple-element.54), custom_call_target="InvertDiagBlocksLowerTriangular" | custom-call | tf_op jit(solution)/shard_map/jit(cholesky)/cholesky | solution.py:10
  416.4 11.9 %cholesky.255 = f32[128,128]{1,0:T(8,128)S(1)} custom-call(f32[128,128]{1,0:T(8,128)S(1)} %convolution_subtract_fusion.6), custom_call_target="Cholesky" | custom-call | tf_op jit(solution)/shard_map/jit(cholesky)/cholesky | solution.py:10
  433.4 10.0 %while.1 = (s32[]{:T(128)}, f32[512,512]{1,0:T(8,128)S(1)}, s32[4,2]{0,1:T(2,128)S(1)}, f32[4,128,128]{2,1,0:T(8,128)}, s32[]{:T(128)}) while((s32[]{:T(128)}, f32[512,512]{1,0:T(8,128)S(1)}, s32[4,2]{0,1:T(2,128)S(1)}, f32[4,128,128]{2,1,0:T(8,128)}, s32[]{:T(128)}) %tuple.93), condition=%wide.while_cond, body=%wide.while_body.sunk | while | flops 2 | bytes 132205 | solution.py:12
  434.0 1.9 bitcast_dynamic-update-slice_fusion.2
  436.5 1.9 bitcast_dynamic-update-slice_fusion.2
  439.0 1.9 bitcast_dynamic-update-slice_fusion.2
  441.5 1.9 bitcast_dynamic-update-slice_fusion.2
  443.4 40.1 %custom-call.35 = f32[4,128,128]{1,2,0:T(8,128)S(1)} custom-call(f32[4,128,128]{2,1,0:T(8,128)} %get-tuple-element.13), custom_call_target="InvertDiagBlocksLowerTriangular" | custom-call | tf_op jit(solution)/shard_map/triangular_solve | solution.py:12
  484.2 1.5 fusion.39
  485.7 1.6 convolution_subtract_fusion.3
  496.0 2.6 add_convert_fusion
  498.6 73.1 %reduce-scatter.2.cloned.1.call-done = f32[32,1024]{1,0:T(8,128)} async-done(((f32[1024,1024]{1,0:T(8,128)}), f32[32,1024]{1,0:T(8,128)}) %reduce-scatter.2.cloned.1.call-update) | async-done | bytes 131088 | tf_op jit(solution)/shard_map/reduce_scatter | solution.py:58
  571.7 2.2 fusion.24
  (87 shorter events, 25.3 us)
Async XLA Ops:
  7.2 109.7 %all-gather.3.cloned.1.call-start = ((), (), s32[]{:S(2)}) async-start(), calls=%async_computation.2 | async-start | bytes 7569408 | tf_op jit(solution)/shard_map/all_gather | solution.py:49
  12.8 11.8 %copy-start.4 = (bf16[32,1024]{1,0:T(8,128)(2,1)S(1)}, bf16[32,1024]{1,0:T(8,128)(2,1)}, u32[]{:S(2)}) copy-start(bf16[32,1024]{1,0:T(8,128)(2,1)} %param.10) | copy-start | bytes 196612
  12.8 11.8 %copy-start.5 = (bf16[32,1024]{1,0:T(8,128)(2,1)S(1)}, bf16[32,1024]{1,0:T(8,128)(2,1)}, u32[]{:S(2)}) copy-start(bf16[32,1024]{1,0:T(8,128)(2,1)} %param.9) | copy-start | bytes 196612
  12.8 12.6 %copy-start.6 = (s32[32]{0:T(128)S(1)}, s32[32]{0:T(128)}, u32[]{:S(2)}) copy-start(s32[32]{0:T(128)} %param.6) | copy-start | bytes 388
  12.8 172.7 %all-to-all-start = ((bf16[32,32,896]{2,0,1:T(8,128)(2,1)}), bf16[32,32,896]{2,0,1:T(8,128)(2,1)S(1)}, u32[]{:S(2)}, u32[]{:S(2)}) async-start(bf16[32,32,896]{2,0,1:T(8,128)(2,1)} %bitcast.118), calls=%async_computation | async-start | bytes 3670016 | tf_op jit(solution)/shard_map/all_to_all | solution.py:48
  24.6 171.6 %all-gather.5.cloned.1.call-start = ((), (), s32[]{:S(2)}) async-start(), calls=%async_computation.4 | async-start | bytes 2162688 | tf_op jit(solution)/shard_map/all_gather | solution.py:63
  25.4 320.8 %all-reduce.4.cloned.1.call-start = ((), (), s32[]{:S(2)}) async-start(), calls=%async_computation.3 | async-start | bytes 2097152 | tf_op jit(solution)/shard_map/psum | solution.py:54
  185.5 2.8 copy-start.2
  188.3 383.4 %reduce-scatter.2.cloned.1.call-start = ((), (), s32[]{:S(2)}) async-start(), calls=%async_computation.5 | async-start | bytes 4325376 | tf_op jit(solution)/shard_map/reduce_scatter | solution.py:58
  347.8 1.2 copy-start
  484.2 3.8 copy-start.1
  494.2 1.7 copy-start.3
  494.2 1.8 copy-start.7
  496.0 75.7 %copy-start.8 = (pred[32]{0:T(512)(128)(4,1)S(1)}, pred[32]{0:T(512)(128)(4,1)}, u32[]{:S(2)}) copy-start(pred[32]{0:T(512)(128)(4,1)} %compare_and_fusion) | copy-start | bytes 100
Sparse Core Ops, SparseCore 0:
  11.5 105.2 all-gather.2
  120.0 75.1 all-gather.4
  198.7 147.3 all-reduce.3
  349.9 221.8 reduce-scatter.1

commit v2 on v1

--- a/solution.py
+++ b/solution.py
@@ -20,6 +20,18 @@
 
 def pick(select, values):
     return jnp.dot(select, values, preferred_element_type=jnp.float32).astype(values.dtype)
+
+
+def gather_rows(x, axis):
+    n = lax.axis_size(axis)
+    copies = jnp.broadcast_to(x[None], (n,) + x.shape)
+    return lax.all_to_all(copies, axis, 0, 0, tiled=True).reshape((n * x.shape[0],) + x.shape[1:])
+
+
+def scatter_rows_sum(x, axis):
+    n = lax.axis_size(axis)
+    parts = lax.all_to_all(x.reshape((n, x.shape[0] // n) + x.shape[1:]), axis, 0, 0, tiled=True)
+    return parts.sum(0)
 
 
 def per_device(counts, keys, inverse_cov, hidden, targets, down_weight):
@@ -50,12 +62,12 @@
     keys_c = pick(select, gathered)
     columns_c = pick(select, columns)
     partial_q = jnp.dot(keys_c, inverse_cov, preferred_element_type=jnp.float32)
-    precond_c = lax.psum(partial_q, "tensor").astype(jnp.bfloat16)
-    gram_c = lax.psum(rows_product(precond_c, columns_c), "dp")
+    precond_c = gather_rows(scatter_rows_sum(partial_q, "tensor").astype(jnp.bfloat16), "tensor")
+    gram_c = gather_rows(scatter_rows_sum(rows_product(precond_c, columns_c), "dp"), "dp")
 
     base_partial = rows_product(columns, down_weight)
     gram_c, base_partial = lax.optimization_barrier((gram_c, base_partial))
-    base = lax.psum_scatter(base_partial, "dp", scatter_dimension=0, tiled=True)
+    base = scatter_rows_sum(base_partial, "dp")
 
     system = gram_c + jnp.eye(live_total, dtype=jnp.float32)
     change = (targets.astype(jnp.float32) - hidden.astype(jnp.float32)) / LAYERS_LEFT

time: 589 us -> 481 us (0.82)
  waiting for transfers between devices: 286 us -> 168 us
  starting transfers between devices: 12.1 us -> 32.3 us
  blocking collectives: 54.6 us -> 35.6 us
    psum x1 -> x0, waiting for transfers between devices: 145 us -> none  [per_device(): gram_c = lax.psum(rows_product(precond_c, columns_c), 'dp')]
    reduce_scatter x1 -> x0, waiting for transfers between devices: 73.1 us -> none  [per_device(): base = lax.psum_scatter(base_partial, 'dp', scatter_dimension=0, tiled=True)]
    psum x1 -> x0, blocking collectives: 54.6 us -> none  [per_device(): precond_c = lax.psum(partial_q, 'tensor').astype(jnp.bfloat16)]
    all_to_all x1, waiting for transfers between devices: 0.01 us -> 40.3 us  [per_device(): lax.all_to_all(masked_keys, 'dp', split_axis=1, concat_axis=0, tiled=True)]
    all_to_all x0 -> x4, waiting for transfers between devices: none -> 36.7 us  [the longest x2 23.1 us: scatter_rows_sum(): lax.all_to_all(x.reshape((n, x.shape[0] // n) + x.shape[1:]), axis, 0, 0,...]
    all_to_all x0 -> x1, blocking collectives: none -> 35.6 us  [scatter_rows_sum(): lax.all_to_all(x.reshape((n, x.shape[0] // n) + x.shape[1:]), axis, 0, 0,...]
    all_to_all x0 -> x4, starting transfers between devices: none -> 25 us  [the longest x2 13.9 us: scatter_rows_sum(): lax.all_to_all(x.reshape((n, x.shape[0] // n) + x.shape[1:]), axis, 0, 0,...]
    all_gather x1, waiting for transfers between devices: 0.01 us -> 18.4 us  [per_device(): resid_all = lax.all_gather(resid_local, 'dp', axis=0, tiled=True)]
  transfers between devices with their start and end apart: 5 -> 7, of which waited for: 3 -> 5; matrix products, arithmetic and copies ran while one was open for 35% -> 38% of each run, Pallas kernels for 0% -> 0%
where the time goes in v2:
time: 481 us; the launch traced here: 471 us
  waiting for transfers between devices  168 us (35%)
  other arithmetic  151 us (31%)
  matrix products  45.3 us (9%)
  blocking collectives  35.6 us (7%)
  starting transfers between devices  32.3 us (7%)
  local copies, waits for them, and re-layouts  21.9 us (5%)
  between operations  17.3 us (4%)
    another operation x14, other arithmetic, cholesky_solve(): factor = jnp.linalg.cholesky(system)  78.8 us
    all_gather x1, waiting for transfers between devices, per_device(): gathered = lax.all_gather(column_part, 'dp', axis=0, tiled=True)  72.6 us
    another operation x3, other arithmetic, cholesky_solve(): lax.linalg.triangular_solve(factor, middle, left_side=True, lower=True, t...  41 us
    all_to_all x1, waiting for transfers between devices, per_device(): lax.all_to_all(masked_keys, 'dp', split_axis=1, concat_axis=0, tiled=True)  40.3 us
    all_to_all x1, blocking collectives, scatter_rows_sum(): lax.all_to_all(x.reshape((n, x.shape[0] // n) + x.shape[1:]), axis, 0, 0,...  35.6 us
    all_to_all x2, waiting for transfers between devices, scatter_rows_sum(): lax.all_to_all(x.reshape((n, x.shape[0] // n) + x.shape[1:]), axis, 0, 0,...  23.1 us
    all_gather x1, waiting for transfers between devices, per_device(): resid_all = lax.all_gather(resid_local, 'dp', axis=0, tiled=True)  18.4 us
    sub x1, other arithmetic, per_device(): row_of = owner * slot_count + compact - starts[owner]  15.8 us
  transfers between devices with their start and end apart: 7, of which 5 were waited for; matrix products, arithmetic and copies ran while one was open for 38% of the time, Pallas kernels for 0%

profile of v2, /device:TPU:2, one launch (start us, length us, event | category | flops | bytes accessed | tf_op | source)
XLA Modules:
  0.0 471.4 jit_solution(1860161568016126076)
XLA Ops:
  13.5 4.4 compare_select_fusion.1
  18.0 15.8 %select_subtract_fusion = s32[512]{0:T(512)S(1)} fusion(pred[512]{0:T(512)(128)(4,1)S(1)} %get-tuple-element.38, pred[512]{0:T(512)(128)(4,1)S(1)} %get-tuple-element.37, pred[512]{0:T(512)(128)(4,1)S(1)} %get-tuple-element.36, pred[512]{0:T(512)(128)(4,1)S(1)} %get-tuple-element.35, pred[512]{0:T(512)(128)(4,1)S(1)} %get-tuple-element.34, ...), kind=kLoop, calls=%fused_computation.144 | loop fusion | flops 14848 | bytes 19044 | tf_op jit(solution)/shard_map/sub | solution.py:50
  33.8 72.6 %all-gather.3.cloned.1.call-done = bf16[1024,3584]{1,0:T(8,128)(2,1)} async-done(((bf16[32,3584]{1,0:T(8,128)(2,1)}), bf16[1024,3584]{1,0:T(8,128)(2,1)}) %all-gather.3.cloned.1.call-update) | async-done | bytes 7340048 | tf_op jit(solution)/shard_map/all_gather | solution.py:61
  106.4 14.0 %fusion.36 = f32[512,896]{1,0:T(8,128)} fusion(bf16[3584,896]{1,0:T(8,128)(2,1)} %param.8, bf16[1024,3584]{1,0:T(8,128)(2,1)} %all-gather.3.cloned.1.call-done, s32[512]{0:T(512)S(1)} %select_subtract_fusion), kind=kOutput, calls=%fused_computation.57 | convolution fusion | flops 7048790016 | bytes 15599616 | tf_op jit(solution)/shard_map/dot_general | solution.py:64
  120.4 4.3 all-to-all-start
  126.1 23.1 %all-to-all-done = f32[8,64,896]{2,1,0:T(8,128)} async-done(((f32[8,64,896]{2,1,0:T(8,128)}), f32[8,64,896]{2,1,0:T(8,128)}, u32[]{:S(2)}, u32[]{:S(2)}) %all-to-all-start) | async-done | bytes 1835040 | tf_op jit(solution)/shard_map/all_to_all | solution.py:33
  149.1 7.3 %all-to-all-start.2 = ((bf16[32,32,896]{2,0,1:T(8,128)(2,1)}), bf16[32,32,896]{2,0,1:T(8,128)(2,1)S(1)}, u32[]{:S(2)}, u32[]{:S(2)}) async-start(bf16[32,32,896]{2,0,1:T(8,128)(2,1)} %bitcast.127), calls=%async_computation.2 | async-start | bytes 3670016 | tf_op jit(solution)/shard_map/all_to_all | solution.py:60
  158.0 40.3 %all-to-all-done.2 = bf16[32,32,896]{2,0,1:T(8,128)(2,1)S(1)} async-done(((bf16[32,32,896]{2,0,1:T(8,128)(2,1)}), bf16[32,32,896]{2,0,1:T(8,128)(2,1)S(1)}, u32[]{:S(2)}, u32[]{:S(2)}) %all-to-all-start.2) | async-done | bytes 1835040 | tf_op jit(solution)/shard_map/all_to_all | solution.py:60
  199.5 3.6 all-to-all-start.1
  203.8 13.7 %all-to-all-done.1 = bf16[8,64,896]{2,1,0:T(8,128)(2,1)S(1)} async-done(((bf16[8,64,896]{2,1,0:T(8,128)(2,1)}), bf16[8,64,896]{2,1,0:T(8,128)(2,1)S(1)}, u32[]{:S(2)}, u32[]{:S(2)}) %all-to-all-start.1) | async-done | bytes 917536 | tf_op jit(solution)/shard_map/all_to_all | solution.py:28
  218.4 3.0 fusion.37
  221.4 35.6 %all_to_all.44 = f32[32,16,512]{2,1,0:T(8,128)S(1)} all-to-all(f32[32,16,512]{2,1,0:T(8,128)S(1)} %fusion.37), channel_id=1, replica_groups=mesh['dp'=32,'tensor'=8] {'dp'}, dimensions={0} | all-to-all | bytes 2097152 | tf_op jit(solution)/shard_map/all_to_all | solution.py:33
  258.2 7.5 %all-to-all-start.4 = ((f32[32,16,512]{2,1,0:T(8,128)}), f32[32,16,512]{2,1,0:T(8,128)S(1)}, u32[]{:S(2)}, u32[]{:S(2)}) async-start(f32[32,16,512]{2,1,0:T(8,128)} %broadcast_in_dim.73), calls=%async_computation.4 | async-start | bytes 2097152 | tf_op jit(solution)/shard_map/all_to_all | solution.py:28
  269.3 6.3 %fusion.88 = f32[1024,1024]{1,0:T(8,128)} fusion(bf16[1024,896]{1,0:T(8,128)(2,1)} %bitcast.131, bf16[1024,896]{1,0:T(8,128)(2,1)} %param.11), kind=kOutput, calls=%fused_computation.175 | convolution fusion | flops 1879048192 | bytes 7864320 | tf_op jit(solution)/shard_map/dot_general | solution.py:16
  275.6 18.4 %all-gather.5.cloned.1.call-done = bf16[1024,1024]{1,0:T(8,128)(2,1)} async-done(((bf16[32,1024]{1,0:T(8,128)(2,1)}), bf16[1024,1024]{1,0:T(8,128)(2,1)}) %all-gather.5.cloned.1.call-update) | async-done | bytes 2097168 | tf_op jit(solution)/shard_map/all_gather | solution.py:75
  294.0 4.5 fusion.84
  300.6 11.7 %cholesky.104 = f32[128,128]{1,0:T(8,128)S(1)} custom-call(f32[128,128]{1,0:T(8,128)S(1)} %cholesky.266), custom_call_target="Cholesky" | custom-call | tf_op jit(solution)/shard_map/jit(cholesky)/cholesky | solution.py:10
  312.5 9.6 %all-to-all-start.5 = ((f32[32,32,1024]{2,1,0:T(8,128)}), f32[32,32,1024]{2,1,0:T(8,128)}, u32[]{:S(2)}, u32[]{:S(2)}) async-start(f32[32,32,1024]{2,1,0:T(8,128)} %bitcast.128), calls=%async_computation.5 | async-start | bytes 8388608 | tf_op jit(solution)/shard_map/all_to_all | solution.py:33
  322.1 9.8 %custom-call.32 = f32[1,128,128]{1,2,0:T(8,128)S(1)} custom-call(f32[1,128,128]{2,1,0:T(8,128)S(1)} %get-tuple-element.60), custom_call_target="InvertDiagBlocksLowerTriangular" | custom-call | tf_op jit(solution)/shard_map/jit(cholesky)/cholesky | solution.py:10
  332.6 11.7 %cholesky.217 = f32[128,128]{1,0:T(8,128)S(1)} custom-call(f32[128,128]{1,0:T(8,128)S(1)} %cholesky.270), custom_call_target="Cholesky" | custom-call | tf_op jit(solution)/shard_map/jit(cholesky)/cholesky | solution.py:10
  344.4 9.8 %custom-call.33 = f32[1,128,128]{1,2,0:T(8,128)S(1)} custom-call(f32[1,128,128]{2,1,0:T(8,128)S(1)} %get-tuple-element.57), custom_call_target="InvertDiagBlocksLowerTriangular" | custom-call | tf_op jit(solution)/shard_map/jit(cholesky)/cholesky | solution.py:10
  354.9 12.1 %cholesky.238 = f32[128,128]{1,0:T(8,128)S(1)} custom-call(f32[128,128]{1,0:T(8,128)S(1)} %cholesky.275), custom_call_target="Cholesky" | custom-call | tf_op jit(solution)/shard_map/jit(cholesky)/cholesky | solution.py:10
  367.0 9.8 %custom-call.34 = f32[1,128,128]{1,2,0:T(8,128)S(1)} custom-call(f32[1,128,128]{2,1,0:T(8,128)S(1)} %get-tuple-element.54), custom_call_target="InvertDiagBlocksLowerTriangular" | custom-call | tf_op jit(solution)/shard_map/jit(cholesky)/cholesky | solution.py:10
  377.4 11.7 %cholesky.255 = f32[128,128]{1,0:T(8,128)S(1)} custom-call(f32[128,128]{1,0:T(8,128)S(1)} %convolution_subtract_fusion.6), custom_call_target="Cholesky" | custom-call | tf_op jit(solution)/shard_map/jit(cholesky)/cholesky | solution.py:10
  394.5 10.7 %while.1 = (s32[]{:T(128)}, f32[512,512]{1,0:T(8,128)S(1)}, s32[4,2]{0,1:T(2,128)S(1)}, f32[4,128,128]{2,1,0:T(8,128)}, s32[]{:T(128)}) while((s32[]{:T(128)}, f32[512,512]{1,0:T(8,128)S(1)}, s32[4,2]{0,1:T(2,128)S(1)}, f32[4,128,128]{2,1,0:T(8,128)}, s32[]{:T(128)}) %tuple.93), condition=%wide.while_cond, body=%wide.while_body.sunk | while | flops 2 | bytes 132205 | solution.py:12
  395.2 2.0 bitcast_dynamic-update-slice_fusion.2
  397.9 2.0 bitcast_dynamic-update-slice_fusion.2
  400.6 2.0 bitcast_dynamic-update-slice_fusion.2
  403.2 2.0 bitcast_dynamic-update-slice_fusion.2
  405.3 40.3 %custom-call.35 = f32[4,128,128]{1,2,0:T(8,128)S(1)} custom-call(f32[4,128,128]{2,1,0:T(8,128)} %get-tuple-element.13), custom_call_target="InvertDiagBlocksLowerTriangular" | custom-call | tf_op jit(solution)/shard_map/triangular_solve | solution.py:12
  458.0 2.6 add_convert_fusion
  460.6 2.4 reduce_sum.39
  (99 shorter events, 40.1 us)
Async XLA Ops:
  7.2 99.2 %all-gather.3.cloned.1.call-start = ((), (), s32[]{:S(2)}) async-start(), calls=%async_computation.6 | async-start | bytes 7569408 | tf_op jit(solution)/shard_map/all_gather | solution.py:61
  9.2 2.4 copy-start.8
  120.4 28.8 %all-to-all-start = ((f32[8,64,896]{2,1,0:T(8,128)}), f32[8,64,896]{2,1,0:T(8,128)}, u32[]{:S(2)}, u32[]{:S(2)}) async-start(f32[8,64,896]{2,1,0:T(8,128)} %bitcast.132), calls=%async_computation | async-start | bytes 3670016 | tf_op jit(solution)/shard_map/all_to_all | solution.py:33
  149.1 49.2 %all-to-all-start.2 = ((bf16[32,32,896]{2,0,1:T(8,128)(2,1)}), bf16[32,32,896]{2,0,1:T(8,128)(2,1)S(1)}, u32[]{:S(2)}, u32[]{:S(2)}) async-start(bf16[32,32,896]{2,0,1:T(8,128)(2,1)} %bitcast.127), calls=%async_computation.2 | async-start | bytes 3670016 | tf_op jit(solution)/shard_map/all_to_all | solution.py:60
  156.4 46.7 %copy-start.6 = (bf16[32,1024]{1,0:T(8,128)(2,1)S(1)}, bf16[32,1024]{1,0:T(8,128)(2,1)}, u32[]{:S(2)}) copy-start(bf16[32,1024]{1,0:T(8,128)(2,1)} %param.10) | copy-start | bytes 196612
  156.4 46.7 %copy-start.7 = (bf16[32,1024]{1,0:T(8,128)(2,1)S(1)}, bf16[32,1024]{1,0:T(8,128)(2,1)}, u32[]{:S(2)}) copy-start(bf16[32,1024]{1,0:T(8,128)(2,1)} %param.9) | copy-start | bytes 196612
  198.3 20.1 %copy-start.2 = (bf16[32,32,896]{2,0,1:T(8,128)(2,1)}, bf16[32,32,896]{2,0,1:T(8,128)(2,1)S(1)}, u32[]{:S(2)}) copy-start(bf16[32,32,896]{2,0,1:T(8,128)(2,1)S(1)} %all-to-all-done.2) | copy-start | bytes 5505028
  199.5 18.0 %all-to-all-start.1 = ((bf16[8,64,896]{2,1,0:T(8,128)(2,1)}), bf16[8,64,896]{2,1,0:T(8,128)(2,1)S(1)}, u32[]{:S(2)}, u32[]{:S(2)}) async-start(bf16[8,64,896]{2,1,0:T(8,128)(2,1)} %broadcast_in_dim.72), calls=%async_computation.1 | async-start | bytes 1835008 | tf_op jit(solution)/shard_map/all_to_all | solution.py:28
  203.0 91.0 %all-gather.5.cloned.1.call-start = ((), (), s32[]{:S(2)}) async-start(), calls=%async_computation.7 | async-start | bytes 2162688 | tf_op jit(solution)/shard_map/all_gather | solution.py:75
  217.5 0.9 copy-start.4
  258.2 40.4 %all-to-all-start.4 = ((f32[32,16,512]{2,1,0:T(8,128)}), f32[32,16,512]{2,1,0:T(8,128)S(1)}, u32[]{:S(2)}, u32[]{:S(2)}) async-start(f32[32,16,512]{2,1,0:T(8,128)} %broadcast_in_dim.73), calls=%async_computation.4 | async-start | bytes 2097152 | tf_op jit(solution)/shard_map/all_to_all | solution.py:28
  299.6 1.0 copy-start
  312.5 19.5 %copy-start.1 = (f32[512,512]{1,0:T(8,128)S(1)}, f32[512,512]{1,0:T(8,128)}, u32[]{:S(2)}) copy-start(f32[512,512]{1,0:T(8,128)} %copy-done) | copy-start | bytes 3145732
  312.5 148.1 %all-to-all-start.5 = ((f32[32,32,1024]{2,1,0:T(8,128)}), f32[32,32,1024]{2,1,0:T(8,128)}, u32[]{:S(2)}, u32[]{:S(2)}) async-start(f32[32,32,1024]{2,1,0:T(8,128)} %bitcast.128), calls=%async_computation.5 | async-start | bytes 8388608 | tf_op jit(solution)/shard_map/all_to_all | solution.py:33
  446.2 3.8 copy-start.3
  456.2 1.7 copy-start.5
  456.2 1.8 copy-start.9
  460.6 2.4 copy-start.10
Sparse Core Ops, SparseCore 0:
  11.8 94.5 all-gather.2
  207.0 87.0 all-gather.4

commit v3 on v2

--- a/solution.py
+++ b/solution.py
@@ -59,6 +59,10 @@
     column_part = lax.dynamic_slice_in_dim(masked_keys, tensor_index * width_part, width_part, 1)
     columns = lax.all_to_all(masked_keys, "dp", split_axis=1, concat_axis=0, tiled=True)
     gathered = lax.all_gather(column_part, "dp", axis=0, tiled=True)
+    change = (targets.astype(jnp.float32) - hidden.astype(jnp.float32)) / LAYERS_LEFT
+    resid_local = jnp.where(live_slot, change, jnp.zeros_like(change)).astype(jnp.bfloat16)
+    resid_all = gather_rows(resid_local, "dp")
+    gathered, columns, resid_all = lax.optimization_barrier((gathered, columns, resid_all))
     keys_c = pick(select, gathered)
     columns_c = pick(select, columns)
     partial_q = jnp.dot(keys_c, inverse_cov, preferred_element_type=jnp.float32)
@@ -70,9 +74,6 @@
     base = scatter_rows_sum(base_partial, "dp")
 
     system = gram_c + jnp.eye(live_total, dtype=jnp.float32)
-    change = (targets.astype(jnp.float32) - hidden.astype(jnp.float32)) / LAYERS_LEFT
-    resid_local = jnp.where(live_slot, change, jnp.zeros_like(change)).astype(jnp.bfloat16)
-    resid_all = lax.all_gather(resid_local, "dp", axis=0, tiled=True)
     resid_c = pick(select, resid_all)
     solved_c = cholesky_solve(system, resid_c.astype(jnp.float32)).astype(jnp.bfloat16)
     weight_delta = lax.dot_general(

time: 481 us -> 471 us (0.979)
  waiting for transfers between devices: 168 us -> 116 us
  blocking collectives: 35.6 us -> 79.9 us
    all_gather x1, waiting for transfers between devices: 72.6 us -> 5.84 us  [per_device(): gathered = lax.all_gather(column_part, 'dp', axis=0, tiled=True)]
    all_to_all x2, waiting for transfers between devices: 13.7 us -> 59.6 us  [gather_rows(): lax.all_to_all(copies, axis, 0, 0, tiled=True)]
    all_to_all x1 -> x2, blocking collectives: 35.6 us -> 62.1 us  [scatter_rows_sum(): lax.all_to_all(x.reshape((n, x.shape[0] // n) + x.shape[1:]), axis, 0, 0,...]
    all_to_all x2 -> x1, waiting for transfers between devices: 23.1 us -> 0.01 us  [scatter_rows_sum(): lax.all_to_all(x.reshape((n, x.shape[0] // n) + x.shape[1:]), axis, 0, 0,...]
    all_gather x1 -> x0, waiting for transfers between devices: 18.4 us -> none  [per_device(): resid_all = lax.all_gather(resid_local, 'dp', axis=0, tiled=True)]
    all_to_all x0 -> x1, blocking collectives: none -> 17.8 us  [gather_rows(): lax.all_to_all(copies, axis, 0, 0, tiled=True)]
    all_to_all x1, waiting for transfers between devices: 40.3 us -> 50.7 us  [per_device(): lax.all_to_all(masked_keys, 'dp', split_axis=1, concat_axis=0, tiled=True)]
    all_to_all x2 -> x1, starting transfers between devices: 13.9 us -> 7.78 us  [scatter_rows_sum(): lax.all_to_all(x.reshape((n, x.shape[0] // n) + x.shape[1:]), axis, 0, 0,...]
  transfers between devices with their start and end apart: 7 -> 5, of which waited for: 5 -> 4; matrix products, arithmetic and copies ran while one was open for 38% -> 37% of each run, Pallas kernels for 0% -> 0%
where the time goes in v3:
time: 471 us; the launch traced here: 463 us
  other arithmetic  148 us (31%)
  waiting for transfers between devices  116 us (25%)
  blocking collectives  79.9 us (17%)
  matrix products  43.4 us (9%)
  starting transfers between devices  36 us (8%)
  local copies, waits for them, and re-layouts  21.7 us (5%)
  between operations  17.6 us (4%)
    another operation x14, other arithmetic, cholesky_solve(): factor = jnp.linalg.cholesky(system)  78.8 us
    all_to_all x2, blocking collectives, scatter_rows_sum(): lax.all_to_all(x.reshape((n, x.shape[0] // n) + x.shape[1:]), axis, 0, 0,...  62.1 us
    all_to_all x2, waiting for transfers between devices, gather_rows(): lax.all_to_all(copies, axis, 0, 0, tiled=True)  59.6 us
    all_to_all x1, waiting for transfers between devices, per_device(): lax.all_to_all(masked_keys, 'dp', split_axis=1, concat_axis=0, tiled=True)  50.7 us
    another operation x3, other arithmetic, cholesky_solve(): lax.linalg.triangular_solve(factor, middle, left_side=True, lower=True, t...  41 us
    all_to_all x1, blocking collectives, gather_rows(): lax.all_to_all(copies, axis, 0, 0, tiled=True)  17.8 us
    all_to_all x2, starting transfers between devices, gather_rows(): lax.all_to_all(copies, axis, 0, 0, tiled=True)  16.5 us
    sub x1, other arithmetic, per_device(): row_of = owner * slot_count + compact - starts[owner]  15.7 us
  transfers between devices with their start and end apart: 5, of which 4 were waited for; matrix products, arithmetic and copies ran while one was open for 37% of the time, Pallas kernels for 0%

profile of v3, /device:TPU:2, one launch (start us, length us, event | category | flops | bytes accessed | tf_op | source)
XLA Modules:
  0.0 463.1 jit_solution(10761843325788685569)
XLA Ops:
  12.9 11.7 %all-to-all-start = ((bf16[32,32,896]{2,0,1:T(8,128)(2,1)}), bf16[32,32,896]{2,0,1:T(8,128)(2,1)S(1)}, u32[]{:S(2)}, u32[]{:S(2)}) async-start(bf16[32,32,896]{2,0,1:T(8,128)(2,1)} %bitcast.128), calls=%async_computation | async-start | bytes 3670016 | tf_op jit(solution)/shard_map/all_to_all | solution.py:60
  24.8 50.7 %all-to-all-done = bf16[32,32,896]{2,0,1:T(8,128)(2,1)S(1)} async-done(((bf16[32,32,896]{2,0,1:T(8,128)(2,1)}), bf16[32,32,896]{2,0,1:T(8,128)(2,1)S(1)}, u32[]{:S(2)}, u32[]{:S(2)}) %all-to-all-start) | async-done | bytes 1835040 | tf_op jit(solution)/shard_map/all_to_all | solution.py:60
  77.4 8.4 %all-to-all-start.1 = ((bf16[32,32,1024]{2,1,0:T(8,128)(2,1)}), bf16[32,32,1024]{2,1,0:T(8,128)(2,1)S(1)}, u32[]{:S(2)}, u32[]{:S(2)}) async-start(bf16[32,32,1024]{2,1,0:T(8,128)(2,1)} %broadcast_in_dim.79), calls=%async_computation.1 | async-start | bytes 4194304 | tf_op jit(solution)/shard_map/all_to_all | solution.py:28
  87.6 4.3 compare_select_fusion.1
  92.0 15.7 %select_subtract_fusion = s32[512]{0:T(512)S(1)} fusion(pred[512]{0:T(512)(128)(4,1)S(1)} %get-tuple-element.44, pred[512]{0:T(512)(128)(4,1)S(1)} %get-tuple-element.43, pred[512]{0:T(512)(128)(4,1)S(1)} %get-tuple-element.42, pred[512]{0:T(512)(128)(4,1)S(1)} %get-tuple-element.41, pred[512]{0:T(512)(128)(4,1)S(1)} %get-tuple-element.40, ...), kind=kLoop, calls=%fused_computation.144 | loop fusion | flops 14848 | bytes 19044 | tf_op jit(solution)/shard_map/sub | solution.py:50
  107.7 46.4 %all-to-all-done.1 = bf16[32,32,1024]{2,1,0:T(8,128)(2,1)S(1)} async-done(((bf16[32,32,1024]{2,1,0:T(8,128)(2,1)}), bf16[32,32,1024]{2,1,0:T(8,128)(2,1)S(1)}, u32[]{:S(2)}, u32[]{:S(2)}) %all-to-all-start.1) | async-done | bytes 2097184 | tf_op jit(solution)/shard_map/all_to_all | solution.py:28
  154.1 5.8 %all-gather.2.cloned.1.call-done = bf16[1024,3584]{1,0:T(8,128)(2,1)} async-done(((bf16[32,3584]{1,0:T(8,128)(2,1)}), bf16[1024,3584]{1,0:T(8,128)(2,1)}) %all-gather.2.cloned.1.call-update) | async-done | bytes 7340048 | tf_op jit(solution)/shard_map/all_gather | solution.py:61
  159.9 14.0 %fusion.36 = f32[512,896]{1,0:T(8,128)} fusion(bf16[3584,896]{1,0:T(8,128)(2,1)} %param.8, bf16[1024,3584]{1,0:T(8,128)(2,1)} %all-gather.2.cloned.1.call-done, s32[512]{0:T(512)S(1)} %select_subtract_fusion), kind=kOutput, calls=%fused_computation.57 | convolution fusion | flops 7048790016 | bytes 15599616 | tf_op jit(solution)/shard_map/dot_general | solution.py:68
  173.9 28.7 %all_to_all.49 = f32[8,64,896]{2,1,0:T(8,128)S(1)} all-to-all(f32[8,64,896]{2,1,0:T(8,128)} %bitcast.134), channel_id=1, replica_groups=mesh['dp'=32,'tensor'=8] {'tensor'}, dimensions={0} | all-to-all | bytes 3670016 | tf_op jit(solution)/shard_map/all_to_all | solution.py:33
  202.8 17.8 %all_to_all.50 = bf16[8,64,896]{2,1,0:T(8,128)(2,1)} all-to-all(bf16[8,64,896]{2,1,0:T(8,128)(2,1)S(1)} %broadcast_in_dim.80), channel_id=1, replica_groups=mesh['dp'=32,'tensor'=8] {'tensor'}, dimensions={0} | all-to-all | bytes 1835008 | tf_op jit(solution)/shard_map/all_to_all | solution.py:28
  220.6 3.0 fusion.37
  223.7 33.4 %all_to_all.51 = f32[32,16,512]{2,1,0:T(8,128)S(1)} all-to-all(f32[32,16,512]{2,1,0:T(8,128)S(1)} %fusion.37), channel_id=1, replica_groups=mesh['dp'=32,'tensor'=8] {'dp'}, dimensions={0} | all-to-all | bytes 2097152 | tf_op jit(solution)/shard_map/all_to_all | solution.py:33
  258.2 8.1 %all-to-all-start.5 = ((f32[32,16,512]{2,1,0:T(8,128)}), f32[32,16,512]{2,1,0:T(8,128)S(1)}, u32[]{:S(2)}, u32[]{:S(2)}) async-start(f32[32,16,512]{2,1,0:T(8,128)} %broadcast_in_dim.81), calls=%async_computation.5 | async-start | bytes 2097152 | tf_op jit(solution)/shard_map/all_to_all | solution.py:28
  269.7 4.7 %fusion.84 = (f32[512,1024]{1,0:T(8,128)}, bf16[512,1024]{1,0:T(8,128)(2,1)}) fusion(bf16[1024,1024]{1,0:T(8,128)(2,1)} %bitcast.131, s32[512]{0:T(512)S(1)} %select_subtract_fusion), kind=kOutput, calls=%fused_computation.171 | convolution fusion | flops 1075314688 | bytes 5244928 | tf_op jit(solution)/shard_map/dot_general | solution.py:22
  274.4 4.4 fusion.88
  278.8 13.3 %all-to-all-done.5 = f32[32,16,512]{2,1,0:T(8,128)S(1)} async-done(((f32[32,16,512]{2,1,0:T(8,128)}), f32[32,16,512]{2,1,0:T(8,128)S(1)}, u32[]{:S(2)}, u32[]{:S(2)}) %all-to-all-start.5) | async-done | bytes 1048608 | tf_op jit(solution)/shard_map/all_to_all | solution.py:28
  294.0 11.7 %cholesky.104 = f32[128,128]{1,0:T(8,128)S(1)} custom-call(f32[128,128]{1,0:T(8,128)S(1)} %cholesky.266), custom_call_target="Cholesky" | custom-call | tf_op jit(solution)/shard_map/jit(cholesky)/cholesky | solution.py:10
  305.9 7.8 %all-to-all-start.6 = ((f32[32,32,1024]{2,1,0:T(8,128)}), f32[32,32,1024]{2,1,0:T(8,128)}, u32[]{:S(2)}, u32[]{:S(2)}) async-start(f32[32,32,1024]{2,1,0:T(8,128)} %bitcast.129), calls=%async_computation.6 | async-start | bytes 8388608 | tf_op jit(solution)/shard_map/all_to_all | solution.py:33
  313.7 9.8 %custom-call.32 = f32[1,128,128]{1,2,0:T(8,128)S(1)} custom-call(f32[1,128,128]{2,1,0:T(8,128)S(1)} %get-tuple-element.66), custom_call_target="InvertDiagBlocksLowerTriangular" | custom-call | tf_op jit(solution)/shard_map/jit(cholesky)/cholesky | solution.py:10
  324.2 11.7 %cholesky.217 = f32[128,128]{1,0:T(8,128)S(1)} custom-call(f32[128,128]{1,0:T(8,128)S(1)} %cholesky.270), custom_call_target="Cholesky" | custom-call | tf_op jit(solution)/shard_map/jit(cholesky)/cholesky | solution.py:10
  336.0 9.8 %custom-call.33 = f32[1,128,128]{1,2,0:T(8,128)S(1)} custom-call(f32[1,128,128]{2,1,0:T(8,128)S(1)} %get-tuple-element.63), custom_call_target="InvertDiagBlocksLowerTriangular" | custom-call | tf_op jit(solution)/shard_map/jit(cholesky)/cholesky | solution.py:10
  346.4 11.9 %cholesky.238 = f32[128,128]{1,0:T(8,128)S(1)} custom-call(f32[128,128]{1,0:T(8,128)S(1)} %cholesky.275), custom_call_target="Cholesky" | custom-call | tf_op jit(solution)/shard_map/jit(cholesky)/cholesky | solution.py:10
  358.4 9.8 %custom-call.34 = f32[1,128,128]{1,2,0:T(8,128)S(1)} custom-call(f32[1,128,128]{2,1,0:T(8,128)S(1)} %get-tuple-element.60), custom_call_target="InvertDiagBlocksLowerTriangular" | custom-call | tf_op jit(solution)/shard_map/jit(cholesky)/cholesky | solution.py:10
  368.8 11.7 %cholesky.255 = f32[128,128]{1,0:T(8,128)S(1)} custom-call(f32[128,128]{1,0:T(8,128)S(1)} %convolution_subtract_fusion.6), custom_call_target="Cholesky" | custom-call | tf_op jit(solution)/shard_map/jit(cholesky)/cholesky | solution.py:10
  386.1 10.5 %while.1 = (s32[]{:T(128)}, f32[512,512]{1,0:T(8,128)S(1)}, s32[4,2]{0,1:T(2,128)S(1)}, f32[4,128,128]{2,1,0:T(8,128)}, s32[]{:T(128)}) while((s32[]{:T(128)}, f32[512,512]{1,0:T(8,128)S(1)}, s32[4,2]{0,1:T(2,128)S(1)}, f32[4,128,128]{2,1,0:T(8,128)}, s32[]{:T(128)}) %tuple.95), condition=%wide.while_cond, body=%wide.while_body.sunk | while | flops 2 | bytes 132205 | solution.py:12
  386.8 2.0 bitcast_dynamic-update-slice_fusion.2
  389.4 2.0 bitcast_dynamic-update-slice_fusion.2
  392.1 2.0 bitcast_dynamic-update-slice_fusion.2
  394.7 2.0 bitcast_dynamic-update-slice_fusion.2
  396.7 40.4 %custom-call.35 = f32[4,128,128]{1,2,0:T(8,128)S(1)} custom-call(f32[4,128,128]{2,1,0:T(8,128)} %get-tuple-element.19), custom_call_target="InvertDiagBlocksLowerTriangular" | custom-call | tf_op jit(solution)/shard_map/triangular_solve | solution.py:12
  449.5 2.6 add_convert_fusion
  452.1 2.4 reduce_sum.39
  (103 shorter events, 37.8 us)
Async XLA Ops:
  7.2 152.8 %all-gather.2.cloned.1.call-start = ((), (), s32[]{:S(2)}) async-start(), calls=%async_computation.7 | async-start | bytes 7569408 | tf_op jit(solution)/shard_map/all_gather | solution.py:61
  12.9 11.8 %copy-start.8 = (bf16[32,1024]{1,0:T(8,128)(2,1)S(1)}, bf16[32,1024]{1,0:T(8,128)(2,1)}, u32[]{:S(2)}) copy-start(bf16[32,1024]{1,0:T(8,128)(2,1)} %param.10) | copy-start | bytes 196612
  12.9 11.8 %copy-start.9 = (bf16[32,1024]{1,0:T(8,128)(2,1)S(1)}, bf16[32,1024]{1,0:T(8,128)(2,1)}, u32[]{:S(2)}) copy-start(bf16[32,1024]{1,0:T(8,128)(2,1)} %param.9) | copy-start | bytes 196612
  12.9 62.5 %all-to-all-start = ((bf16[32,32,896]{2,0,1:T(8,128)(2,1)}), bf16[32,32,896]{2,0,1:T(8,128)(2,1)S(1)}, u32[]{:S(2)}, u32[]{:S(2)}) async-start(bf16[32,32,896]{2,0,1:T(8,128)(2,1)} %bitcast.128), calls=%async_computation | async-start | bytes 3670016 | tf_op jit(solution)/shard_map/all_to_all | solution.py:60
  75.4 1.9 copy-start.3
  77.2 8.5 %copy-start.10 = (s32[32]{0:T(128)S(1)}, s32[32]{0:T(128)}, u32[]{:S(2)}) copy-start(s32[32]{0:T(128)} %param.6) | copy-start | bytes 388
  77.4 76.7 %all-to-all-start.1 = ((bf16[32,32,1024]{2,1,0:T(8,128)(2,1)}), bf16[32,32,1024]{2,1,0:T(8,128)(2,1)S(1)}, u32[]{:S(2)}, u32[]{:S(2)}) async-start(bf16[32,32,1024]{2,1,0:T(8,128)(2,1)} %broadcast_in_dim.79), calls=%async_computation.1 | async-start | bytes 4194304 | tf_op jit(solution)/shard_map/all_to_all | solution.py:28
  154.1 19.8 %copy-start.2 = (bf16[32,32,1024]{2,1,0:T(8,128)(2,1)}, bf16[32,32,1024]{2,1,0:T(8,128)(2,1)S(1)}, u32[]{:S(2)}) copy-start(bf16[32,32,1024]{2,1,0:T(8,128)(2,1)S(1)} %all-to-all-done.1) | copy-start | bytes 6291460
  202.7 17.9 %copy-start.4 = (bf16[32,32,896]{2,0,1:T(8,128)(2,1)S(1)}, bf16[32,32,896]{2,0,1:T(8,128)(2,1)}, u32[]{:S(2)}) copy-start(bf16[32,32,896]{2,0,1:T(8,128)(2,1)} %copy-done.3) | copy-start | bytes 5505028
  258.2 33.8 %all-to-all-start.5 = ((f32[32,16,512]{2,1,0:T(8,128)}), f32[32,16,512]{2,1,0:T(8,128)S(1)}, u32[]{:S(2)}, u32[]{:S(2)}) async-start(f32[32,16,512]{2,1,0:T(8,128)} %broadcast_in_dim.81), calls=%async_computation.5 | async-start | bytes 2097152 | tf_op jit(solution)/shard_map/all_to_all | solution.py:28
  269.7 4.7 %copy-start.5 = (bf16[32,32,896]{2,0,1:T(8,128)(2,1)S(1)}, bf16[32,32,896]{2,0,1:T(8,128)(2,1)}, u32[]{:S(2)}) copy-start(bf16[32,32,896]{2,0,1:T(8,128)(2,1)} %copy-done.3) | copy-start | bytes 5505028
  269.7 4.7 %copy-start.11 = (bf16[1024,896]{1,0:T(8,128)(2,1)S(1)}, bf16[1024,896]{1,0:T(8,128)(2,1)}, u32[]{:S(2)}) copy-start(bf16[1024,896]{1,0:T(8,128)(2,1)} %param.11) | copy-start | bytes 5505028
  293.0 1.0 copy-start
  305.9 17.6 %copy-start.1 = (f32[512,512]{1,0:T(8,128)S(1)}, f32[512,512]{1,0:T(8,128)}, u32[]{:S(2)}) copy-start(f32[512,512]{1,0:T(8,128)} %copy-done) | copy-start | bytes 3145732
  305.9 146.2 %all-to-all-start.6 = ((f32[32,32,1024]{2,1,0:T(8,128)}), f32[32,32,1024]{2,1,0:T(8,128)}, u32[]{:S(2)}, u32[]{:S(2)}) async-start(f32[32,32,1024]{2,1,0:T(8,128)} %bitcast.129), calls=%async_computation.6 | async-start | bytes 8388608 | tf_op jit(solution)/shard_map/all_to_all | solution.py:33
  437.6 3.8 copy-start.6
  447.7 1.7 copy-start.7
  447.7 1.8 copy-start.12
  452.1 2.4 copy-start.13
Sparse Core Ops, SparseCore 0:
  11.6 148.2 all-gather.1

commit v4 on v3

--- a/solution.py
+++ b/solution.py
@@ -61,8 +61,8 @@
     gathered = lax.all_gather(column_part, "dp", axis=0, tiled=True)
     change = (targets.astype(jnp.float32) - hidden.astype(jnp.float32)) / LAYERS_LEFT
     resid_local = jnp.where(live_slot, change, jnp.zeros_like(change)).astype(jnp.bfloat16)
-    resid_all = gather_rows(resid_local, "dp")
-    gathered, columns, resid_all = lax.optimization_barrier((gathered, columns, resid_all))
+    gathered, columns = lax.optimization_barrier((gathered, columns))
+    resid_all = lax.all_gather(resid_local, "dp", axis=0, tiled=True)
     keys_c = pick(select, gathered)
     columns_c = pick(select, columns)
     partial_q = jnp.dot(keys_c, inverse_cov, preferred_element_type=jnp.float32)

time: 471 us -> 445 us (0.945)
  the two profiles are of different devices: /device:TPU:2 before, /device:TPU:26 now
where the time goes in v4:
time: 445 us; the launch traced here: 436 us
  other arithmetic  149 us (33%)
  waiting for transfers between devices  106 us (24%)
  blocking collectives  61.9 us (14%)
  matrix products  43.4 us (10%)
  starting transfers between devices  36.9 us (8%)
  local copies, waits for them, and re-layouts  21.2 us (5%)
  between operations  17.5 us (4%)
    another operation x14, other arithmetic, cholesky_solve(): factor = jnp.linalg.cholesky(system)  78.5 us
    all_to_all x2, blocking collectives, scatter_rows_sum(): lax.all_to_all(x.reshape((n, x.shape[0] // n) + x.shape[1:]), axis, 0, 0,...  61.9 us
    all_gather x1, waiting for transfers between devices, per_device(): gathered = lax.all_gather(column_part, 'dp', axis=0, tiled=True)  41.2 us
    another operation x3, other arithmetic, cholesky_solve(): lax.linalg.triangular_solve(factor, middle, left_side=True, lower=True, t...  41.1 us
    all_to_all x1, waiting for transfers between devices, per_device(): lax.all_to_all(masked_keys, 'dp', split_axis=1, concat_axis=0, tiled=True)  28.5 us
    all_gather x1, waiting for transfers between devices, per_device(): resid_all = lax.all_gather(resid_local, 'dp', axis=0, tiled=True)  24.9 us
    sub x1, other arithmetic, per_device(): row_of = owner * slot_count + compact - starts[owner]  15.8 us
    dot_general x1, matrix products, per_device(): partial_q = jnp.dot(keys_c, inverse_cov, preferred_element_type=jnp.float32)  14 us
  transfers between devices with their start and end apart: 6, of which 4 were waited for; matrix products, arithmetic and copies ran while one was open for 40% of the time, Pallas kernels for 0%

profile of v4, /device:TPU:26, one launch (start us, length us, event | category | flops | bytes accessed | tf_op | source)
XLA Modules:
  0.0 436.4 jit_solution(15875345044955905430)
XLA Ops:
  12.8 11.7 %all-to-all-start = ((bf16[32,32,896]{2,0,1:T(8,128)(2,1)}), bf16[32,32,896]{2,0,1:T(8,128)(2,1)S(1)}, u32[]{:S(2)}, u32[]{:S(2)}) async-start(bf16[32,32,896]{2,0,1:T(8,128)(2,1)} %bitcast.127), calls=%async_computation | async-start | bytes 3670016 | tf_op jit(solution)/shard_map/all_to_all | solution.py:60
  26.4 4.5 %compare_select_fusion.1 = (s32[512,1]{0,1:T(1,128)S(1)}, s32[512,1]{0,1:T(1,128)S(1)}) fusion(s32[]{:T(128)} %bitcast.27, s32[]{:T(128)} %bitcast.28, s32[]{:T(128)} %bitcast.29, s32[]{:T(128)} %bitcast.30, s32[]{:T(128)} %bitcast.31, s32[]{:T(128)} %bitcast.33, s32[]{:T(128)} %bitcast.32, s32[512,1]{0,1:T(1,128)S(1)} %bitcast.136), kind=kLoop, calls=%fused_computation.135 | loop fusion | flops 7680 | bytes 6172 | tf_op jit(solution)/shard_map/gather | solution.py:50
  31.1 15.8 %select_subtract_fusion = s32[512]{0:T(512)S(1)} fusion(pred[512]{0:T(512)(128)(4,1)S(1)} %get-tuple-element.42, pred[512]{0:T(512)(128)(4,1)S(1)} %get-tuple-element.41, pred[512]{0:T(512)(128)(4,1)S(1)} %get-tuple-element.40, pred[512]{0:T(512)(128)(4,1)S(1)} %get-tuple-element.39, pred[512]{0:T(512)(128)(4,1)S(1)} %get-tuple-element.38, ...), kind=kLoop, calls=%fused_computation.144 | loop fusion | flops 14848 | bytes 19044 | tf_op jit(solution)/shard_map/sub | solution.py:50
  46.8 28.5 %all-to-all-done = bf16[32,32,896]{2,0,1:T(8,128)(2,1)S(1)} async-done(((bf16[32,32,896]{2,0,1:T(8,128)(2,1)}), bf16[32,32,896]{2,0,1:T(8,128)(2,1)S(1)}, u32[]{:S(2)}, u32[]{:S(2)}) %all-to-all-start) | async-done | bytes 1835040 | tf_op jit(solution)/shard_map/all_to_all | solution.py:60
  75.4 41.2 %all-gather.3.cloned.1.call-done = bf16[1024,3584]{1,0:T(8,128)(2,1)} async-done(((bf16[32,3584]{1,0:T(8,128)(2,1)}), bf16[1024,3584]{1,0:T(8,128)(2,1)}) %all-gather.3.cloned.1.call-update) | async-done | bytes 7340048 | tf_op jit(solution)/shard_map/all_gather | solution.py:61
  116.6 14.0 %fusion.36 = f32[512,896]{1,0:T(8,128)} fusion(bf16[3584,896]{1,0:T(8,128)(2,1)} %param.8, bf16[1024,3584]{1,0:T(8,128)(2,1)} %all-gather.3.cloned.1.call-done, s32[512]{0:T(512)S(1)} %select_subtract_fusion), kind=kOutput, calls=%fused_computation.57 | convolution fusion | flops 7048790016 | bytes 15599616 | tf_op jit(solution)/shard_map/dot_general | solution.py:68
  130.6 27.1 %all_to_all.44 = f32[8,64,896]{2,1,0:T(8,128)S(1)} all-to-all(f32[8,64,896]{2,1,0:T(8,128)} %bitcast.132), channel_id=1, replica_groups=mesh['dp'=32,'tensor'=8] {'tensor'}, dimensions={0} | all-to-all | bytes 3670016 | tf_op jit(solution)/shard_map/all_to_all | solution.py:33
  158.8 5.6 %all-to-all-start.2 = ((bf16[8,64,896]{2,1,0:T(8,128)(2,1)}), bf16[8,64,896]{2,1,0:T(8,128)(2,1)S(1)}, u32[]{:S(2)}, u32[]{:S(2)}) async-start(bf16[8,64,896]{2,1,0:T(8,128)(2,1)} %broadcast_in_dim.72), calls=%async_computation.2 | async-start | bytes 1835008 | tf_op jit(solution)/shard_map/all_to_all | solution.py:28
  165.2 11.7 %all-to-all-done.2 = bf16[8,64,896]{2,1,0:T(8,128)(2,1)S(1)} async-done(((bf16[8,64,896]{2,1,0:T(8,128)(2,1)}), bf16[8,64,896]{2,1,0:T(8,128)(2,1)S(1)}, u32[]{:S(2)}, u32[]{:S(2)}) %all-to-all-start.2) | async-done | bytes 917536 | tf_op jit(solution)/shard_map/all_to_all | solution.py:28
  177.8 3.0 fusion.37
  180.8 34.8 %all_to_all.45 = f32[32,16,512]{2,1,0:T(8,128)S(1)} all-to-all(f32[32,16,512]{2,1,0:T(8,128)S(1)} %fusion.37), channel_id=1, replica_groups=mesh['dp'=32,'tensor'=8] {'dp'}, dimensions={0} | all-to-all | bytes 2097152 | tf_op jit(solution)/shard_map/all_to_all | solution.py:33
  216.8 7.8 %all-to-all-start.4 = ((f32[32,16,512]{2,1,0:T(8,128)}), f32[32,16,512]{2,1,0:T(8,128)S(1)}, u32[]{:S(2)}, u32[]{:S(2)}) async-start(f32[32,16,512]{2,1,0:T(8,128)} %broadcast_in_dim.73), calls=%async_computation.4 | async-start | bytes 2097152 | tf_op jit(solution)/shard_map/all_to_all | solution.py:28
  226.4 1.8 compare_and_fusion
  228.2 24.9 %all-gather.5.cloned.1.call-done = bf16[1024,1024]{1,0:T(8,128)(2,1)} async-done(((bf16[32,1024]{1,0:T(8,128)(2,1)}), bf16[1024,1024]{1,0:T(8,128)(2,1)}) %all-gather.5.cloned.1.call-update) | async-done | bytes 2097168 | tf_op jit(solution)/shard_map/all_gather | solution.py:65
  253.1 4.7 %fusion.84 = (f32[512,1024]{1,0:T(8,128)}, bf16[512,1024]{1,0:T(8,128)(2,1)}) fusion(bf16[1024,1024]{1,0:T(8,128)(2,1)} %all-gather.5.cloned.1.call-done, s32[512]{0:T(512)S(1)} %select_subtract_fusion), kind=kOutput, calls=%fused_computation.171 | convolution fusion | flops 1075314688 | bytes 5244928 | tf_op jit(solution)/shard_map/dot_general | solution.py:22
  257.8 4.3 fusion.88
  264.2 11.7 %cholesky.104 = f32[128,128]{1,0:T(8,128)S(1)} custom-call(f32[128,128]{1,0:T(8,128)S(1)} %cholesky.266), custom_call_target="Cholesky" | custom-call | tf_op jit(solution)/shard_map/jit(cholesky)/cholesky | solution.py:10
  276.0 11.8 %all-to-all-start.5 = ((f32[32,32,1024]{2,1,0:T(8,128)}), f32[32,32,1024]{2,1,0:T(8,128)}, u32[]{:S(2)}, u32[]{:S(2)}) async-start(f32[32,32,1024]{2,1,0:T(8,128)} %bitcast.128), calls=%async_computation.5 | async-start | bytes 8388608 | tf_op jit(solution)/shard_map/all_to_all | solution.py:33
  287.8 9.8 %custom-call.32 = f32[1,128,128]{1,2,0:T(8,128)S(1)} custom-call(f32[1,128,128]{2,1,0:T(8,128)S(1)} %get-tuple-element.64), custom_call_target="InvertDiagBlocksLowerTriangular" | custom-call | tf_op jit(solution)/shard_map/jit(cholesky)/cholesky | solution.py:10
  298.3 11.7 %cholesky.217 = f32[128,128]{1,0:T(8,128)S(1)} custom-call(f32[128,128]{1,0:T(8,128)S(1)} %cholesky.270), custom_call_target="Cholesky" | custom-call | tf_op jit(solution)/shard_map/jit(cholesky)/cholesky | solution.py:10
  310.0 9.8 %custom-call.33 = f32[1,128,128]{1,2,0:T(8,128)S(1)} custom-call(f32[1,128,128]{2,1,0:T(8,128)S(1)} %get-tuple-element.61), custom_call_target="InvertDiagBlocksLowerTriangular" | custom-call | tf_op jit(solution)/shard_map/jit(cholesky)/cholesky | solution.py:10
  320.5 11.9 %cholesky.238 = f32[128,128]{1,0:T(8,128)S(1)} custom-call(f32[128,128]{1,0:T(8,128)S(1)} %cholesky.275), custom_call_target="Cholesky" | custom-call | tf_op jit(solution)/shard_map/jit(cholesky)/cholesky | solution.py:10
  332.5 9.8 %custom-call.34 = f32[1,128,128]{1,2,0:T(8,128)S(1)} custom-call(f32[1,128,128]{2,1,0:T(8,128)S(1)} %get-tuple-element.58), custom_call_target="InvertDiagBlocksLowerTriangular" | custom-call | tf_op jit(solution)/shard_map/jit(cholesky)/cholesky | solution.py:10
  342.9 11.7 %cholesky.255 = f32[128,128]{1,0:T(8,128)S(1)} custom-call(f32[128,128]{1,0:T(8,128)S(1)} %convolution_subtract_fusion.6), custom_call_target="Cholesky" | custom-call | tf_op jit(solution)/shard_map/jit(cholesky)/cholesky | solution.py:10
  359.9 10.1 %while.1 = (s32[]{:T(128)}, f32[512,512]{1,0:T(8,128)S(1)}, s32[4,2]{0,1:T(2,128)S(1)}, f32[4,128,128]{2,1,0:T(8,128)}, s32[]{:T(128)}) while((s32[]{:T(128)}, f32[512,512]{1,0:T(8,128)S(1)}, s32[4,2]{0,1:T(2,128)S(1)}, f32[4,128,128]{2,1,0:T(8,128)}, s32[]{:T(128)}) %tuple.95), condition=%wide.while_cond, body=%wide.while_body.sunk | while | flops 2 | bytes 132205 | solution.py:12
  360.5 1.9 bitcast_dynamic-update-slice_fusion.2
  363.0 1.9 bitcast_dynamic-update-slice_fusion.2
  365.5 1.9 bitcast_dynamic-update-slice_fusion.2
  368.0 1.9 bitcast_dynamic-update-slice_fusion.2
  370.0 40.4 %custom-call.35 = f32[4,128,128]{1,2,0:T(8,128)S(1)} custom-call(f32[4,128,128]{2,1,0:T(8,128)} %get-tuple-element.17), custom_call_target="InvertDiagBlocksLowerTriangular" | custom-call | tf_op jit(solution)/shard_map/triangular_solve | solution.py:12
  422.8 2.6 add_convert_fusion
  425.4 2.4 reduce_sum.39
  (104 shorter events, 36.2 us)
Async XLA Ops:
  7.2 109.5 %all-gather.3.cloned.1.call-start = ((), (), s32[]{:S(2)}) async-start(), calls=%async_computation.6 | async-start | bytes 7569408 | tf_op jit(solution)/shard_map/all_gather | solution.py:61
  12.8 11.8 %copy-start.10 = (s32[32]{0:T(128)S(1)}, s32[32]{0:T(128)}, u32[]{:S(2)}) copy-start(s32[32]{0:T(128)} %param.6) | copy-start | bytes 388
  12.8 62.5 %all-to-all-start = ((bf16[32,32,896]{2,0,1:T(8,128)(2,1)}), bf16[32,32,896]{2,0,1:T(8,128)(2,1)S(1)}, u32[]{:S(2)}, u32[]{:S(2)}) async-start(bf16[32,32,896]{2,0,1:T(8,128)(2,1)} %bitcast.127), calls=%async_computation | async-start | bytes 3670016 | tf_op jit(solution)/shard_map/all_to_all | solution.py:60
  75.4 55.2 %copy-start.2 = (bf16[32,32,896]{2,0,1:T(8,128)(2,1)}, bf16[32,32,896]{2,0,1:T(8,128)(2,1)S(1)}, u32[]{:S(2)}) copy-start(bf16[32,32,896]{2,0,1:T(8,128)(2,1)S(1)} %all-to-all-done) | copy-start | bytes 5505028
  157.7 6.7 %copy-start.8 = (bf16[32,1024]{1,0:T(8,128)(2,1)S(1)}, bf16[32,1024]{1,0:T(8,128)(2,1)}, u32[]{:S(2)}) copy-start(bf16[32,1024]{1,0:T(8,128)(2,1)} %param.10) | copy-start | bytes 196612
  157.7 6.7 %copy-start.9 = (bf16[32,1024]{1,0:T(8,128)(2,1)S(1)}, bf16[32,1024]{1,0:T(8,128)(2,1)}, u32[]{:S(2)}) copy-start(bf16[32,1024]{1,0:T(8,128)(2,1)} %param.9) | copy-start | bytes 196612
  157.8 20.0 %copy-start.3 = (bf16[32,32,896]{2,0,1:T(8,128)(2,1)S(1)}, bf16[32,32,896]{2,0,1:T(8,128)(2,1)}, u32[]{:S(2)}) copy-start(bf16[32,32,896]{2,0,1:T(8,128)(2,1)} %copy-done.2) | copy-start | bytes 5505028
  158.8 18.0 %all-to-all-start.2 = ((bf16[8,64,896]{2,1,0:T(8,128)(2,1)}), bf16[8,64,896]{2,1,0:T(8,128)(2,1)S(1)}, u32[]{:S(2)}, u32[]{:S(2)}) async-start(bf16[8,64,896]{2,1,0:T(8,128)(2,1)} %broadcast_in_dim.72), calls=%async_computation.2 | async-start | bytes 1835008 | tf_op jit(solution)/shard_map/all_to_all | solution.py:28
  164.4 88.7 %all-gather.5.cloned.1.call-start = ((), (), s32[]{:S(2)}) async-start(), calls=%async_computation.7 | async-start | bytes 2162688 | tf_op jit(solution)/shard_map/all_gather | solution.py:65
  176.8 0.9 copy-start.6
  216.8 45.3 %all-to-all-start.4 = ((f32[32,16,512]{2,1,0:T(8,128)}), f32[32,16,512]{2,1,0:T(8,128)S(1)}, u32[]{:S(2)}, u32[]{:S(2)}) async-start(f32[32,16,512]{2,1,0:T(8,128)} %broadcast_in_dim.73), calls=%async_computation.4 | async-start | bytes 2097152 | tf_op jit(solution)/shard_map/all_to_all | solution.py:28
  253.1 4.7 %copy-start.4 = (bf16[32,32,896]{2,0,1:T(8,128)(2,1)S(1)}, bf16[32,32,896]{2,0,1:T(8,128)(2,1)}, u32[]{:S(2)}) copy-start(bf16[32,32,896]{2,0,1:T(8,128)(2,1)} %copy-done.2) | copy-start | bytes 5505028
  253.1 4.7 %copy-start.11 = (bf16[1024,896]{1,0:T(8,128)(2,1)S(1)}, bf16[1024,896]{1,0:T(8,128)(2,1)}, u32[]{:S(2)}) copy-start(bf16[1024,896]{1,0:T(8,128)(2,1)} %param.11) | copy-start | bytes 5505028
  263.1 1.0 copy-start
  276.0 21.6 %copy-start.1 = (f32[512,512]{1,0:T(8,128)S(1)}, f32[512,512]{1,0:T(8,128)}, u32[]{:S(2)}) copy-start(f32[512,512]{1,0:T(8,128)} %copy-done) | copy-start | bytes 3145732
  276.0 149.4 %all-to-all-start.5 = ((f32[32,32,1024]{2,1,0:T(8,128)}), f32[32,32,1024]{2,1,0:T(8,128)}, u32[]{:S(2)}, u32[]{:S(2)}) async-start(f32[32,32,1024]{2,1,0:T(8,128)} %bitcast.128), calls=%async_computation.5 | async-start | bytes 8388608 | tf_op jit(solution)/shard_map/all_to_all | solution.py:33
  410.9 3.8 copy-start.5
  421.0 1.7 copy-start.7
  421.0 1.8 copy-start.12
  425.4 2.4 copy-start.13
Sparse Core Ops, SparseCore 0:
  11.6 104.9 all-gather.2
  168.4 84.6 all-gather.4

commit v5 on v4

--- a/solution.py
+++ b/solution.py
@@ -74,8 +74,13 @@
     base = scatter_rows_sum(base_partial, "dp")
 
     system = gram_c + jnp.eye(live_total, dtype=jnp.float32)
+    factor = jnp.linalg.cholesky(system)
+    factor, resid_all = lax.optimization_barrier((factor, resid_all))
     resid_c = pick(select, resid_all)
-    solved_c = cholesky_solve(system, resid_c.astype(jnp.float32)).astype(jnp.bfloat16)
+    middle = lax.linalg.triangular_solve(factor, resid_c.astype(jnp.float32), left_side=True, lower=True)
+    solved_c = lax.linalg.triangular_solve(
+        factor, middle, left_side=True, lower=True, transpose_a=True
+    ).astype(jnp.bfloat16)
     weight_delta = lax.dot_general(
         solved_c, precond_c, (((0,), (0,)), ((), ())), preferred_element_type=jnp.float32
     )

time: 445 us -> 428 us (0.962)
  the two profiles are of different devices: /device:TPU:26 before, /device:TPU:2 now
where the time goes in v5:
time: 428 us; the launch traced here: 420 us
  other arithmetic  150 us (35%)
  waiting for transfers between devices  85.3 us (20%)
  blocking collectives  79.7 us (19%)
  matrix products  42.6 us (10%)
  starting transfers between devices  27.2 us (6%)
  local copies, waits for them, and re-layouts  18.4 us (4%)
  between operations  17.3 us (4%)
    another operation x14, other arithmetic, per_device(): factor = jnp.linalg.cholesky(system)  78.9 us
    all_to_all x2, blocking collectives, scatter_rows_sum(): lax.all_to_all(x.reshape((n, x.shape[0] // n) + x.shape[1:]), axis, 0, 0,...  61.9 us
    all_gather x1, waiting for transfers between devices, per_device(): gathered = lax.all_gather(column_part, 'dp', axis=0, tiled=True)  41.5 us
    another operation x3, other arithmetic, per_device(): lax.linalg.triangular_solve(factor, middle, left_side=True, lower=True, t...  40.8 us
    all_to_all x1, waiting for transfers between devices, per_device(): lax.all_to_all(masked_keys, 'dp', split_axis=1, concat_axis=0, tiled=True)  28.5 us
    all_to_all x1, blocking collectives, gather_rows(): lax.all_to_all(copies, axis, 0, 0, tiled=True)  17.8 us
    sub x1, other arithmetic, per_device(): row_of = owner * slot_count + compact - starts[owner]  15.8 us
    all_to_all x1, waiting for transfers between devices, gather_rows(): lax.all_to_all(copies, axis, 0, 0, tiled=True)  15.2 us
  transfers between devices with their start and end apart: 5, of which 3 were waited for; matrix products, arithmetic and copies ran while one was open for 44% of the time, Pallas kernels for 0%

profile of v5, /device:TPU:2, one launch (start us, length us, event | category | flops | bytes accessed | tf_op | source)
XLA Modules:
  0.0 420.0 jit_solution(14050498017757439736)
XLA Ops:
  9.1 1.7 broadcast_select_fusion
  13.0 11.7 %all-to-all-start = ((bf16[32,32,896]{2,0,1:T(8,128)(2,1)}), bf16[32,32,896]{2,0,1:T(8,128)(2,1)S(1)}, u32[]{:S(2)}, u32[]{:S(2)}) async-start(bf16[32,32,896]{2,0,1:T(8,128)(2,1)} %bitcast.127), calls=%async_computation | async-start | bytes 3670016 | tf_op jit(solution)/shard_map/all_to_all | solution.py:60
  26.5 4.5 %compare_select_fusion.1 = (s32[512,1]{0,1:T(1,128)S(1)}, s32[512,1]{0,1:T(1,128)S(1)}) fusion(s32[]{:T(128)} %bitcast.27, s32[]{:T(128)} %bitcast.28, s32[]{:T(128)} %bitcast.29, s32[]{:T(128)} %bitcast.30, s32[]{:T(128)} %bitcast.31, s32[]{:T(128)} %bitcast.33, s32[]{:T(128)} %bitcast.32, s32[512,1]{0,1:T(1,128)S(1)} %bitcast.136), kind=kLoop, calls=%fused_computation.136 | loop fusion | flops 7680 | bytes 6172 | tf_op jit(solution)/shard_map/gather | solution.py:50
  31.2 15.8 %select_subtract_fusion = s32[512]{0:T(512)S(1)} fusion(pred[512]{0:T(512)(128)(4,1)S(1)} %get-tuple-element.46, pred[512]{0:T(512)(128)(4,1)S(1)} %get-tuple-element.45, pred[512]{0:T(512)(128)(4,1)S(1)} %get-tuple-element.44, pred[512]{0:T(512)(128)(4,1)S(1)} %get-tuple-element.43, pred[512]{0:T(512)(128)(4,1)S(1)} %get-tuple-element.42, ...), kind=kLoop, calls=%fused_computation.145 | loop fusion | flops 14848 | bytes 19044 | tf_op jit(solution)/shard_map/sub | solution.py:50
  47.0 28.5 %all-to-all-done = bf16[32,32,896]{2,0,1:T(8,128)(2,1)S(1)} async-done(((bf16[32,32,896]{2,0,1:T(8,128)(2,1)}), bf16[32,32,896]{2,0,1:T(8,128)(2,1)S(1)}, u32[]{:S(2)}, u32[]{:S(2)}) %all-to-all-start) | async-done | bytes 1835040 | tf_op jit(solution)/shard_map/all_to_all | solution.py:60
  75.5 41.5 %all-gather.3.cloned.1.call-done = bf16[1024,3584]{1,0:T(8,128)(2,1)} async-done(((bf16[32,3584]{1,0:T(8,128)(2,1)}), bf16[1024,3584]{1,0:T(8,128)(2,1)}) %all-gather.3.cloned.1.call-update) | async-done | bytes 7340048 | tf_op jit(solution)/shard_map/all_gather | solution.py:61
  117.0 14.0 %fusion.37 = f32[512,896]{1,0:T(8,128)} fusion(bf16[3584,896]{1,0:T(8,128)(2,1)} %param.8, bf16[1024,3584]{1,0:T(8,128)(2,1)} %all-gather.3.cloned.1.call-done, s32[512]{0:T(512)S(1)} %select_subtract_fusion), kind=kOutput, calls=%fused_computation.58 | convolution fusion | flops 7048790016 | bytes 15599616 | tf_op jit(solution)/shard_map/dot_general | solution.py:68
  130.9 28.7 %all_to_all.44 = f32[8,64,896]{2,1,0:T(8,128)S(1)} all-to-all(f32[8,64,896]{2,1,0:T(8,128)} %bitcast.132), channel_id=1, replica_groups=mesh['dp'=32,'tensor'=8] {'tensor'}, dimensions={0} | all-to-all | bytes 3670016 | tf_op jit(solution)/shard_map/all_to_all | solution.py:33
  159.8 17.8 %all_to_all.45 = bf16[8,64,896]{2,1,0:T(8,128)(2,1)} all-to-all(bf16[8,64,896]{2,1,0:T(8,128)(2,1)S(1)} %broadcast_in_dim.72), channel_id=1, replica_groups=mesh['dp'=32,'tensor'=8] {'tensor'}, dimensions={0} | all-to-all | bytes 1835008 | tf_op jit(solution)/shard_map/all_to_all | solution.py:28
  177.6 4.0 fusion.38
  181.6 33.2 %all_to_all.46 = f32[32,16,512]{2,1,0:T(8,128)S(1)} all-to-all(f32[32,16,512]{2,1,0:T(8,128)} %fusion.38), channel_id=1, replica_groups=mesh['dp'=32,'tensor'=8] {'dp'}, dimensions={0} | all-to-all | bytes 2097152 | tf_op jit(solution)/shard_map/all_to_all | solution.py:33
  216.0 7.5 %all-to-all-start.4 = ((f32[32,16,512]{2,1,0:T(8,128)}), f32[32,16,512]{2,1,0:T(8,128)S(1)}, u32[]{:S(2)}, u32[]{:S(2)}) async-start(f32[32,16,512]{2,1,0:T(8,128)} %broadcast_in_dim.73), calls=%async_computation.4 | async-start | bytes 2097152 | tf_op jit(solution)/shard_map/all_to_all | solution.py:28
  226.4 1.8 compare_and_fusion
  228.3 6.5 %fusion.89 = f32[1024,1024]{1,0:T(8,128)} fusion(bf16[1024,896]{1,0:T(8,128)(2,1)} %bitcast.130, bf16[1024,896]{1,0:T(8,128)(2,1)} %param.11), kind=kOutput, calls=%fused_computation.176 | convolution fusion | flops 1879048192 | bytes 7864320 | tf_op jit(solution)/shard_map/dot_general | solution.py:16
  234.7 15.2 %all-to-all-done.4 = f32[32,16,512]{2,1,0:T(8,128)S(1)} async-done(((f32[32,16,512]{2,1,0:T(8,128)}), f32[32,16,512]{2,1,0:T(8,128)S(1)}, u32[]{:S(2)}, u32[]{:S(2)}) %all-to-all-start.4) | async-done | bytes 1048608 | tf_op jit(solution)/shard_map/all_to_all | solution.py:28
  251.0 11.7 %cholesky.104 = f32[128,128]{1,0:T(8,128)S(1)} custom-call(f32[128,128]{1,0:T(8,128)S(1)} %cholesky.266), custom_call_target="Cholesky" | custom-call | tf_op jit(solution)/shard_map/jit(cholesky)/cholesky | solution.py:77
  262.9 9.8 %custom-call.32 = f32[1,128,128]{1,2,0:T(8,128)S(1)} custom-call(f32[1,128,128]{2,1,0:T(8,128)S(1)} %get-tuple-element.68), custom_call_target="InvertDiagBlocksLowerTriangular" | custom-call | tf_op jit(solution)/shard_map/jit(cholesky)/cholesky | solution.py:77
  273.4 12.1 %cholesky.217 = f32[128,128]{1,0:T(8,128)S(1)} custom-call(f32[128,128]{1,0:T(8,128)S(1)} %cholesky.270), custom_call_target="Cholesky" | custom-call | tf_op jit(solution)/shard_map/jit(cholesky)/cholesky | solution.py:77
  285.5 7.6 %all-to-all-start.5 = ((f32[32,32,1024]{2,1,0:T(8,128)}), f32[32,32,1024]{2,1,0:T(8,128)}, u32[]{:S(2)}, u32[]{:S(2)}) async-start(f32[32,32,1024]{2,1,0:T(8,128)} %bitcast.128), calls=%async_computation.5 | async-start | bytes 8388608 | tf_op jit(solution)/shard_map/all_to_all | solution.py:33
  293.2 9.8 %custom-call.33 = f32[1,128,128]{1,2,0:T(8,128)S(1)} custom-call(f32[1,128,128]{2,1,0:T(8,128)S(1)} %get-tuple-element.65), custom_call_target="InvertDiagBlocksLowerTriangular" | custom-call | tf_op jit(solution)/shard_map/jit(cholesky)/cholesky | solution.py:77
  303.6 11.7 %cholesky.238 = f32[128,128]{1,0:T(8,128)S(1)} custom-call(f32[128,128]{1,0:T(8,128)S(1)} %cholesky.275), custom_call_target="Cholesky" | custom-call | tf_op jit(solution)/shard_map/jit(cholesky)/cholesky | solution.py:77
  315.4 9.8 %custom-call.34 = f32[1,128,128]{1,2,0:T(8,128)S(1)} custom-call(f32[1,128,128]{2,1,0:T(8,128)S(1)} %get-tuple-element.62), custom_call_target="InvertDiagBlocksLowerTriangular" | custom-call | tf_op jit(solution)/shard_map/jit(cholesky)/cholesky | solution.py:77
  325.8 11.9 %cholesky.255 = f32[128,128]{1,0:T(8,128)S(1)} custom-call(f32[128,128]{1,0:T(8,128)S(1)} %convolution_subtract_fusion.6), custom_call_target="Cholesky" | custom-call | tf_op jit(solution)/shard_map/jit(cholesky)/cholesky | solution.py:77
  342.9 10.4 %while.1 = (s32[]{:T(128)}, f32[512,512]{1,0:T(8,128)S(1)}, s32[4,2]{0,1:T(2,128)S(1)}, f32[4,128,128]{2,1,0:T(8,128)}, s32[]{:T(128)}) while((s32[]{:T(128)}, f32[512,512]{1,0:T(8,128)S(1)}, s32[4,2]{0,1:T(2,128)S(1)}, f32[4,128,128]{2,1,0:T(8,128)}, s32[]{:T(128)}) %tuple.97), condition=%wide.while_cond, body=%wide.while_body.sunk | while | flops 2 | bytes 132705 | solution.py:81
  343.5 2.0 bitcast_dynamic-update-slice_fusion.2
  346.1 2.0 bitcast_dynamic-update-slice_fusion.2
  348.7 2.0 bitcast_dynamic-update-slice_fusion.2
  351.3 2.0 bitcast_dynamic-update-slice_fusion.2
  353.3 40.1 %custom-call.35 = f32[4,128,128]{1,2,0:T(8,128)S(1)} custom-call(f32[4,128,128]{2,1,0:T(8,128)} %get-tuple-element.21), custom_call_target="InvertDiagBlocksLowerTriangular" | custom-call | tf_op jit(solution)/shard_map/triangular_solve | solution.py:81
  394.1 2.9 fusion.85
  406.7 2.6 add_convert_fusion
  409.2 2.4 reduce_sum.39
  (98 shorter events, 29.8 us)
Async XLA Ops:
  7.2 109.8 %all-gather.3.cloned.1.call-start = ((), (), s32[]{:S(2)}) async-start(), calls=%async_computation.6 | async-start | bytes 7569408 | tf_op jit(solution)/shard_map/all_gather | solution.py:61
  9.1 214.7 %copy-start.5 = (pred[32]{0:T(512)(128)(4,1)}, pred[32]{0:T(512)(128)(4,1)S(1)}, u32[]{:S(2)}) copy-start(pred[32]{0:T(512)(128)(4,1)S(1)} %iota_compare_fusion.19) | copy-start | bytes 100
  13.0 11.8 %copy-start.7 = (s32[32]{0:T(128)S(1)}, s32[32]{0:T(128)}, u32[]{:S(2)}) copy-start(s32[32]{0:T(128)} %param.6) | copy-start | bytes 388
  13.0 62.5 %all-to-all-start = ((bf16[32,32,896]{2,0,1:T(8,128)(2,1)}), bf16[32,32,896]{2,0,1:T(8,128)(2,1)S(1)}, u32[]{:S(2)}, u32[]{:S(2)}) async-start(bf16[32,32,896]{2,0,1:T(8,128)(2,1)} %bitcast.127), calls=%async_computation | async-start | bytes 3670016 | tf_op jit(solution)/shard_map/all_to_all | solution.py:60
  75.5 55.4 %copy-start = (bf16[32,32,896]{2,0,1:T(8,128)(2,1)}, bf16[32,32,896]{2,0,1:T(8,128)(2,1)S(1)}, u32[]{:S(2)}) copy-start(bf16[32,32,896]{2,0,1:T(8,128)(2,1)S(1)} %all-to-all-done) | copy-start | bytes 5505028
  159.7 17.9 %copy-start.1 = (bf16[32,32,896]{2,0,1:T(8,128)(2,1)S(1)}, bf16[32,32,896]{2,0,1:T(8,128)(2,1)}, u32[]{:S(2)}) copy-start(bf16[32,32,896]{2,0,1:T(8,128)(2,1)} %copy-done) | copy-start | bytes 5505028
  214.9 9.0 %copy-start.3 = (bf16[32,1024]{1,0:T(8,128)(2,1)S(1)}, bf16[32,1024]{1,0:T(8,128)(2,1)}, u32[]{:S(2)}) copy-start(bf16[32,1024]{1,0:T(8,128)(2,1)} %param.10) | copy-start | bytes 196612
  214.9 9.0 %copy-start.4 = (bf16[32,1024]{1,0:T(8,128)(2,1)S(1)}, bf16[32,1024]{1,0:T(8,128)(2,1)}, u32[]{:S(2)}) copy-start(bf16[32,1024]{1,0:T(8,128)(2,1)} %param.9) | copy-start | bytes 196612
  216.0 33.9 %all-to-all-start.4 = ((f32[32,16,512]{2,1,0:T(8,128)}), f32[32,16,512]{2,1,0:T(8,128)S(1)}, u32[]{:S(2)}, u32[]{:S(2)}) async-start(f32[32,16,512]{2,1,0:T(8,128)} %broadcast_in_dim.73), calls=%async_computation.4 | async-start | bytes 2097152 | tf_op jit(solution)/shard_map/all_to_all | solution.py:28
  223.6 118.8 %all-gather.5.cloned.1.call-start = ((), (), s32[]{:S(2)}) async-start(), calls=%async_computation.7 | async-start | bytes 2162688 | tf_op jit(solution)/shard_map/all_gather | solution.py:65
  285.5 123.8 %all-to-all-start.5 = ((f32[32,32,1024]{2,1,0:T(8,128)}), f32[32,32,1024]{2,1,0:T(8,128)}, u32[]{:S(2)}, u32[]{:S(2)}) async-start(f32[32,32,1024]{2,1,0:T(8,128)} %bitcast.128), calls=%async_computation.5 | async-start | bytes 8388608 | tf_op jit(solution)/shard_map/all_to_all | solution.py:33
  342.3 0.7 copy-start.10
  404.9 1.7 copy-start.2
  404.9 1.8 copy-start.8
  409.2 2.4 copy-start.6
  409.2 2.5 copy-start.9
Sparse Core Ops, SparseCore 0:
  11.7 105.2 all-gather.2
  227.6 82.1 all-gather.4

commit v6 on v5

--- a/solution.py
+++ b/solution.py
@@ -62,7 +62,6 @@
     change = (targets.astype(jnp.float32) - hidden.astype(jnp.float32)) / LAYERS_LEFT
     resid_local = jnp.where(live_slot, change, jnp.zeros_like(change)).astype(jnp.bfloat16)
     gathered, columns = lax.optimization_barrier((gathered, columns))
-    resid_all = lax.all_gather(resid_local, "dp", axis=0, tiled=True)
     keys_c = pick(select, gathered)
     columns_c = pick(select, columns)
     partial_q = jnp.dot(keys_c, inverse_cov, preferred_element_type=jnp.float32)
@@ -70,7 +69,8 @@
     gram_c = gather_rows(scatter_rows_sum(rows_product(precond_c, columns_c), "dp"), "dp")
 
     base_partial = rows_product(columns, down_weight)
-    gram_c, base_partial = lax.optimization_barrier((gram_c, base_partial))
+    gram_c, base_partial, resid_local = lax.optimization_barrier((gram_c, base_partial, resid_local))
+    resid_all = lax.all_gather(resid_local, "dp", axis=0, tiled=True)
     base = scatter_rows_sum(base_partial, "dp")
 
     system = gram_c + jnp.eye(live_total, dtype=jnp.float32)

time: 428 us -> 431 us (level)
  transfers between devices with their start and end apart: 5 -> 5, of which waited for: 3 -> 3; matrix products, arithmetic and copies ran while one was open for 44% -> 43% of each run, Pallas kernels for 0% -> 0%
where the time goes in v6:
time: 431 us; the launch traced here: 423 us
  other arithmetic  150 us (35%)
  waiting for transfers between devices  89.1 us (21%)
  blocking collectives  79 us (18%)
  matrix products  40.7 us (9%)
  starting transfers between devices  27 us (6%)
  local copies, waits for them, and re-layouts  19.8 us (5%)
  between operations  17.4 us (4%)
    another operation x14, other arithmetic, per_device(): factor = jnp.linalg.cholesky(system)  79 us
    all_to_all x2, blocking collectives, scatter_rows_sum(): lax.all_to_all(x.reshape((n, x.shape[0] // n) + x.shape[1:]), axis, 0, 0,...  61.9 us
    all_gather x1, waiting for transfers between devices, per_device(): gathered = lax.all_gather(column_part, 'dp', axis=0, tiled=True)  41.4 us
    another operation x3, other arithmetic, per_device(): lax.linalg.triangular_solve(factor, middle, left_side=True, lower=True, t...  40.8 us
    all_to_all x1, waiting for transfers between devices, per_device(): lax.all_to_all(masked_keys, 'dp', split_axis=1, concat_axis=0, tiled=True)  28.6 us
    all_to_all x1, waiting for transfers between devices, gather_rows(): lax.all_to_all(copies, axis, 0, 0, tiled=True)  19 us
    all_to_all x1, blocking collectives, gather_rows(): lax.all_to_all(copies, axis, 0, 0, tiled=True)  17.1 us
    sub x1, other arithmetic, per_device(): row_of = owner * slot_count + compact - starts[owner]  15.7 us
  transfers between devices with their start and end apart: 5, of which 3 were waited for; matrix products, arithmetic and copies ran while one was open for 43% of the time, Pallas kernels for 0%

profile of v6, /device:TPU:2, one launch (start us, length us, event | category | flops | bytes accessed | tf_op | source)
XLA Modules:
  0.0 422.8 jit_solution(1653775005797389685)
XLA Ops:
  9.2 1.7 broadcast_select_fusion
  13.1 11.7 %all-to-all-start = ((bf16[32,32,896]{2,0,1:T(8,128)(2,1)}), bf16[32,32,896]{2,0,1:T(8,128)(2,1)S(1)}, u32[]{:S(2)}, u32[]{:S(2)}) async-start(bf16[32,32,896]{2,0,1:T(8,128)(2,1)} %bitcast.127), calls=%async_computation | async-start | bytes 3670016 | tf_op jit(solution)/shard_map/all_to_all | solution.py:60
  26.6 4.4 %compare_select_fusion.1 = (s32[512,1]{0,1:T(1,128)S(1)}, s32[512,1]{0,1:T(1,128)S(1)}) fusion(s32[]{:T(128)} %bitcast.27, s32[]{:T(128)} %bitcast.28, s32[]{:T(128)} %bitcast.29, s32[]{:T(128)} %bitcast.30, s32[]{:T(128)} %bitcast.31, s32[]{:T(128)} %bitcast.33, s32[]{:T(128)} %bitcast.32, s32[512,1]{0,1:T(1,128)S(1)} %bitcast.136), kind=kLoop, calls=%fused_computation.136 | loop fusion | flops 7680 | bytes 6172 | tf_op jit(solution)/shard_map/gather | solution.py:50
  31.2 15.7 %select_subtract_fusion = s32[512]{0:T(512)S(1)} fusion(pred[512]{0:T(512)(128)(4,1)S(1)} %get-tuple-element.48, pred[512]{0:T(512)(128)(4,1)S(1)} %get-tuple-element.47, pred[512]{0:T(512)(128)(4,1)S(1)} %get-tuple-element.46, pred[512]{0:T(512)(128)(4,1)S(1)} %get-tuple-element.45, pred[512]{0:T(512)(128)(4,1)S(1)} %get-tuple-element.44, ...), kind=kLoop, calls=%fused_computation.145 | loop fusion | flops 14848 | bytes 19044 | tf_op jit(solution)/shard_map/sub | solution.py:50
  47.0 28.6 %all-to-all-done = bf16[32,32,896]{2,0,1:T(8,128)(2,1)S(1)} async-done(((bf16[32,32,896]{2,0,1:T(8,128)(2,1)}), bf16[32,32,896]{2,0,1:T(8,128)(2,1)S(1)}, u32[]{:S(2)}, u32[]{:S(2)}) %all-to-all-start) | async-done | bytes 1835040 | tf_op jit(solution)/shard_map/all_to_all | solution.py:60
  75.6 41.4 %all-gather.3.cloned.1.call-done = bf16[1024,3584]{1,0:T(8,128)(2,1)} async-done(((bf16[32,3584]{1,0:T(8,128)(2,1)}), bf16[1024,3584]{1,0:T(8,128)(2,1)}) %all-gather.3.cloned.1.call-update) | async-done | bytes 7340048 | tf_op jit(solution)/shard_map/all_gather | solution.py:61
  117.0 14.0 %fusion.37 = f32[512,896]{1,0:T(8,128)} fusion(bf16[3584,896]{1,0:T(8,128)(2,1)} %param.8, bf16[1024,3584]{1,0:T(8,128)(2,1)} %all-gather.3.cloned.1.call-done, s32[512]{0:T(512)S(1)} %select_subtract_fusion), kind=kOutput, calls=%fused_computation.58 | convolution fusion | flops 7048790016 | bytes 15599616 | tf_op jit(solution)/shard_map/dot_general | solution.py:67
  131.0 28.7 %all_to_all.44 = f32[8,64,896]{2,1,0:T(8,128)S(1)} all-to-all(f32[8,64,896]{2,1,0:T(8,128)} %bitcast.132), channel_id=1, replica_groups=mesh['dp'=32,'tensor'=8] {'tensor'}, dimensions={0} | all-to-all | bytes 3670016 | tf_op jit(solution)/shard_map/all_to_all | solution.py:33
  159.9 17.1 %all_to_all.45 = bf16[8,64,896]{2,1,0:T(8,128)(2,1)S(1)} all-to-all(bf16[8,64,896]{2,1,0:T(8,128)(2,1)S(1)} %broadcast_in_dim.72), channel_id=1, replica_groups=mesh['dp'=32,'tensor'=8] {'tensor'}, dimensions={0} | all-to-all | bytes 1835008 | tf_op jit(solution)/shard_map/all_to_all | solution.py:28
  177.9 2.8 fusion.38
  180.7 33.2 %all_to_all.46 = f32[32,16,512]{2,1,0:T(8,128)S(1)} all-to-all(f32[32,16,512]{2,1,0:T(8,128)} %fusion.38), channel_id=1, replica_groups=mesh['dp'=32,'tensor'=8] {'dp'}, dimensions={0} | all-to-all | bytes 2097152 | tf_op jit(solution)/shard_map/all_to_all | solution.py:33
  215.1 7.5 %all-to-all-start.4 = ((f32[32,16,512]{2,1,0:T(8,128)}), f32[32,16,512]{2,1,0:T(8,128)S(1)}, u32[]{:S(2)}, u32[]{:S(2)}) async-start(f32[32,16,512]{2,1,0:T(8,128)} %broadcast_in_dim.73), calls=%async_computation.4 | async-start | bytes 2097152 | tf_op jit(solution)/shard_map/all_to_all | solution.py:28
  223.6 5.8 %fusion.89 = f32[1024,1024]{1,0:T(8,128)} fusion(bf16[1024,896]{1,0:T(8,128)(2,1)S(1)} %bitcast.131, bf16[1024,896]{1,0:T(8,128)(2,1)} %param.11), kind=kOutput, calls=%fused_computation.176 | convolution fusion | flops 1879048192 | bytes 7864320 | tf_op jit(solution)/shard_map/dot_general | solution.py:16
  229.4 19.0 %all-to-all-done.4 = f32[32,16,512]{2,1,0:T(8,128)S(1)} async-done(((f32[32,16,512]{2,1,0:T(8,128)}), f32[32,16,512]{2,1,0:T(8,128)S(1)}, u32[]{:S(2)}, u32[]{:S(2)}) %all-to-all-start.4) | async-done | bytes 1048608 | tf_op jit(solution)/shard_map/all_to_all | solution.py:28
  250.4 1.9 compare_and_fusion
  253.3 11.7 %cholesky.104 = f32[128,128]{1,0:T(8,128)S(1)} custom-call(f32[128,128]{1,0:T(8,128)S(1)} %cholesky.266), custom_call_target="Cholesky" | custom-call | tf_op jit(solution)/shard_map/jit(cholesky)/cholesky | solution.py:77
  265.2 9.8 %custom-call.32 = f32[1,128,128]{1,2,0:T(8,128)S(1)} custom-call(f32[1,128,128]{2,1,0:T(8,128)S(1)} %get-tuple-element.70), custom_call_target="InvertDiagBlocksLowerTriangular" | custom-call | tf_op jit(solution)/shard_map/jit(cholesky)/cholesky | solution.py:77
  275.7 12.1 %cholesky.217 = f32[128,128]{1,0:T(8,128)S(1)} custom-call(f32[128,128]{1,0:T(8,128)S(1)} %cholesky.270), custom_call_target="Cholesky" | custom-call | tf_op jit(solution)/shard_map/jit(cholesky)/cholesky | solution.py:77
  287.7 7.5 %all-to-all-start.5 = ((f32[32,32,1024]{2,1,0:T(8,128)}), f32[32,32,1024]{2,1,0:T(8,128)}, u32[]{:S(2)}, u32[]{:S(2)}) async-start(f32[32,32,1024]{2,1,0:T(8,128)} %bitcast.128), calls=%async_computation.5 | async-start | bytes 8388608 | tf_op jit(solution)/shard_map/all_to_all | solution.py:33
  295.3 9.8 %custom-call.33 = f32[1,128,128]{1,2,0:T(8,128)S(1)} custom-call(f32[1,128,128]{2,1,0:T(8,128)S(1)} %get-tuple-element.67), custom_call_target="InvertDiagBlocksLowerTriangular" | custom-call | tf_op jit(solution)/shard_map/jit(cholesky)/cholesky | solution.py:77
  305.8 11.7 %cholesky.238 = f32[128,128]{1,0:T(8,128)S(1)} custom-call(f32[128,128]{1,0:T(8,128)S(1)} %cholesky.275), custom_call_target="Cholesky" | custom-call | tf_op jit(solution)/shard_map/jit(cholesky)/cholesky | solution.py:77
  317.5 9.8 %custom-call.34 = f32[1,128,128]{1,2,0:T(8,128)S(1)} custom-call(f32[1,128,128]{2,1,0:T(8,128)S(1)} %get-tuple-element.64), custom_call_target="InvertDiagBlocksLowerTriangular" | custom-call | tf_op jit(solution)/shard_map/jit(cholesky)/cholesky | solution.py:77
  327.9 11.9 %cholesky.255 = f32[128,128]{1,0:T(8,128)S(1)} custom-call(f32[128,128]{1,0:T(8,128)S(1)} %convolution_subtract_fusion.6), custom_call_target="Cholesky" | custom-call | tf_op jit(solution)/shard_map/jit(cholesky)/cholesky | solution.py:77
  345.9 10.8 %while.1 = (s32[]{:T(128)}, f32[512,512]{1,0:T(8,128)S(1)}, s32[4,2]{0,1:T(2,128)S(1)}, f32[4,128,128]{2,1,0:T(8,128)}, s32[]{:T(128)}) while((s32[]{:T(128)}, f32[512,512]{1,0:T(8,128)S(1)}, s32[4,2]{0,1:T(2,128)S(1)}, f32[4,128,128]{2,1,0:T(8,128)}, s32[]{:T(128)}) %tuple.97), condition=%wide.while_cond, body=%wide.while_body.sunk | while | flops 2 | bytes 132705 | solution.py:81
  346.6 2.1 bitcast_dynamic-update-slice_fusion.2
  349.3 2.1 bitcast_dynamic-update-slice_fusion.2
  352.0 2.1 bitcast_dynamic-update-slice_fusion.2
  354.7 2.1 bitcast_dynamic-update-slice_fusion.2
  356.7 40.1 %custom-call.35 = f32[4,128,128]{1,2,0:T(8,128)S(1)} custom-call(f32[4,128,128]{2,1,0:T(8,128)} %get-tuple-element.23), custom_call_target="InvertDiagBlocksLowerTriangular" | custom-call | tf_op jit(solution)/shard_map/triangular_solve | solution.py:81
  396.9 2.9 fusion.85
  409.5 2.6 add_convert_fusion
  412.0 2.4 reduce_sum.39
  (100 shorter events, 31.3 us)
Async XLA Ops:
  7.2 109.8 %all-gather.3.cloned.1.call-start = ((), (), s32[]{:S(2)}) async-start(), calls=%async_computation.6 | async-start | bytes 7569408 | tf_op jit(solution)/shard_map/all_gather | solution.py:61
  9.2 213.7 %copy-start.6 = (pred[32]{0:T(512)(128)(4,1)}, pred[32]{0:T(512)(128)(4,1)S(1)}, u32[]{:S(2)}) copy-start(pred[32]{0:T(512)(128)(4,1)S(1)} %iota_compare_fusion.19) | copy-start | bytes 100
  13.1 11.8 %copy-start.8 = (s32[32]{0:T(128)S(1)}, s32[32]{0:T(128)}, u32[]{:S(2)}) copy-start(s32[32]{0:T(128)} %param.6) | copy-start | bytes 388
  13.1 62.5 %all-to-all-start = ((bf16[32,32,896]{2,0,1:T(8,128)(2,1)}), bf16[32,32,896]{2,0,1:T(8,128)(2,1)S(1)}, u32[]{:S(2)}, u32[]{:S(2)}) async-start(bf16[32,32,896]{2,0,1:T(8,128)(2,1)} %bitcast.127), calls=%async_computation | async-start | bytes 3670016 | tf_op jit(solution)/shard_map/all_to_all | solution.py:60
  75.6 55.4 %copy-start = (bf16[32,32,896]{2,0,1:T(8,128)(2,1)}, bf16[32,32,896]{2,0,1:T(8,128)(2,1)S(1)}, u32[]{:S(2)}) copy-start(bf16[32,32,896]{2,0,1:T(8,128)(2,1)S(1)} %all-to-all-done) | copy-start | bytes 5505028
  159.7 18.2 %copy-start.1 = (bf16[32,32,896]{2,0,1:T(8,128)(2,1)S(1)}, bf16[32,32,896]{2,0,1:T(8,128)(2,1)}, u32[]{:S(2)}) copy-start(bf16[32,32,896]{2,0,1:T(8,128)(2,1)} %copy-done) | copy-start | bytes 5505028
  177.0 0.9 copy-start.2
  213.9 9.0 %copy-start.4 = (bf16[32,1024]{1,0:T(8,128)(2,1)S(1)}, bf16[32,1024]{1,0:T(8,128)(2,1)}, u32[]{:S(2)}) copy-start(bf16[32,1024]{1,0:T(8,128)(2,1)} %param.10) | copy-start | bytes 196612
  213.9 9.0 %copy-start.5 = (bf16[32,1024]{1,0:T(8,128)(2,1)S(1)}, bf16[32,1024]{1,0:T(8,128)(2,1)}, u32[]{:S(2)}) copy-start(bf16[32,1024]{1,0:T(8,128)(2,1)} %param.9) | copy-start | bytes 196612
  215.1 33.4 %all-to-all-start.4 = ((f32[32,16,512]{2,1,0:T(8,128)}), f32[32,16,512]{2,1,0:T(8,128)S(1)}, u32[]{:S(2)}, u32[]{:S(2)}) async-start(f32[32,16,512]{2,1,0:T(8,128)} %broadcast_in_dim.73), calls=%async_computation.4 | async-start | bytes 2097152 | tf_op jit(solution)/shard_map/all_to_all | solution.py:28
  222.7 122.7 %all-gather.5.cloned.1.call-start = ((), (), s32[]{:S(2)}) async-start(), calls=%async_computation.7 | async-start | bytes 2162688 | tf_op jit(solution)/shard_map/all_gather | solution.py:73
  287.7 124.3 %all-to-all-start.5 = ((f32[32,32,1024]{2,1,0:T(8,128)}), f32[32,32,1024]{2,1,0:T(8,128)}, u32[]{:S(2)}, u32[]{:S(2)}) async-start(f32[32,32,1024]{2,1,0:T(8,128)} %bitcast.128), calls=%async_computation.5 | async-start | bytes 8388608 | tf_op jit(solution)/shard_map/all_to_all | solution.py:33
  345.2 0.7 copy-start.11
  407.7 1.7 copy-start.3
  407.7 1.8 copy-start.9
  412.0 2.4 copy-start.7
  412.0 2.5 copy-start.10
Sparse Core Ops, SparseCore 0:
  11.8 105.1 all-gather.2
  248.6 87.4 all-gather.4

commit v7 on v5

--- a/solution.py
+++ b/solution.py
@@ -66,7 +66,12 @@
     keys_c = pick(select, gathered)
     columns_c = pick(select, columns)
     partial_q = jnp.dot(keys_c, inverse_cov, preferred_element_type=jnp.float32)
-    precond_c = gather_rows(scatter_rows_sum(partial_q, "tensor").astype(jnp.bfloat16), "tensor")
+    tensor_size = lax.axis_size("tensor")
+    parts_q = lax.all_to_all(
+        partial_q.astype(jnp.bfloat16).reshape((tensor_size, -1) + partial_q.shape[1:]),
+        "tensor", 0, 0, tiled=True,
+    ).astype(jnp.float32).sum(0)
+    precond_c = gather_rows(parts_q.astype(jnp.bfloat16), "tensor")
     gram_c = gather_rows(scatter_rows_sum(rows_product(precond_c, columns_c), "dp"), "dp")
 
     base_partial = rows_product(columns, down_weight)

time: 428 us -> 417 us (0.974)
  blocking collectives: 79.7 us -> 69.6 us
    all_to_all x2 -> x1, blocking collectives: 61.9 us -> 33 us  [scatter_rows_sum(): lax.all_to_all(x.reshape((n, x.shape[0] // n) + x.shape[1:]), axis, 0, 0,...]
    all_to_all x0 -> x1, blocking collectives: none -> 18.9 us  [per_device(): lax.all_to_all(partial_q.astype(jnp.bfloat16).reshape((tensor_size, -1) +...]
  transfers between devices with their start and end apart: 5 -> 5, of which waited for: 3 -> 3; matrix products, arithmetic and copies ran while one was open for 44% -> 45% of each run, Pallas kernels for 0% -> 0%
where the time goes in v7:
time: 417 us; the launch traced here: 409 us
  other arithmetic  150 us (36%)
  waiting for transfers between devices  85.5 us (21%)
  blocking collectives  69.6 us (17%)
  matrix products  41.2 us (10%)
  starting transfers between devices  27.2 us (7%)
  local copies, waits for them, and re-layouts  18.3 us (4%)
  between operations  17.3 us (4%)
    another operation x14, other arithmetic, per_device(): factor = jnp.linalg.cholesky(system)  79 us
    all_gather x1, waiting for transfers between devices, per_device(): gathered = lax.all_gather(column_part, 'dp', axis=0, tiled=True)  41.5 us
    another operation x3, other arithmetic, per_device(): lax.linalg.triangular_solve(factor, middle, left_side=True, lower=True, t...  40.8 us
    all_to_all x1, blocking collectives, scatter_rows_sum(): lax.all_to_all(x.reshape((n, x.shape[0] // n) + x.shape[1:]), axis, 0, 0,...  33 us
    all_to_all x1, waiting for transfers between devices, per_device(): lax.all_to_all(masked_keys, 'dp', split_axis=1, concat_axis=0, tiled=True)  28.5 us
    all_to_all x1, blocking collectives, per_device(): lax.all_to_all(partial_q.astype(jnp.bfloat16).reshape((tensor_size, -1) +...  18.9 us
    all_to_all x1, blocking collectives, gather_rows(): lax.all_to_all(copies, axis, 0, 0, tiled=True)  17.7 us
    sub x1, other arithmetic, per_device(): row_of = owner * slot_count + compact - starts[owner]  15.8 us
  transfers between devices with their start and end apart: 5, of which 3 were waited for; matrix products, arithmetic and copies ran while one was open for 45% of the time, Pallas kernels for 0%

profile of v7, /device:TPU:2, one launch (start us, length us, event | category | flops | bytes accessed | tf_op | source)
XLA Modules:
  0.0 408.6 jit_solution(1317642860902086746)
XLA Ops:
  9.0 1.7 broadcast_select_fusion
  12.9 11.7 %all-to-all-start = ((bf16[32,32,896]{2,0,1:T(8,128)(2,1)}), bf16[32,32,896]{2,0,1:T(8,128)(2,1)S(1)}, u32[]{:S(2)}, u32[]{:S(2)}) async-start(bf16[32,32,896]{2,0,1:T(8,128)(2,1)} %bitcast.127), calls=%async_computation | async-start | bytes 3670016 | tf_op jit(solution)/shard_map/all_to_all | solution.py:60
  26.4 4.4 %compare_select_fusion.1 = (s32[512,1]{0,1:T(1,128)S(1)}, s32[512,1]{0,1:T(1,128)S(1)}) fusion(s32[]{:T(128)} %bitcast.27, s32[]{:T(128)} %bitcast.28, s32[]{:T(128)} %bitcast.29, s32[]{:T(128)} %bitcast.30, s32[]{:T(128)} %bitcast.31, s32[]{:T(128)} %bitcast.33, s32[]{:T(128)} %bitcast.32, s32[512,1]{0,1:T(1,128)S(1)} %bitcast.136), kind=kLoop, calls=%fused_computation.136 | loop fusion | flops 7680 | bytes 6172 | tf_op jit(solution)/shard_map/gather | solution.py:50
  31.0 15.8 %select_subtract_fusion = s32[512]{0:T(512)S(1)} fusion(pred[512]{0:T(512)(128)(4,1)S(1)} %get-tuple-element.46, pred[512]{0:T(512)(128)(4,1)S(1)} %get-tuple-element.45, pred[512]{0:T(512)(128)(4,1)S(1)} %get-tuple-element.44, pred[512]{0:T(512)(128)(4,1)S(1)} %get-tuple-element.43, pred[512]{0:T(512)(128)(4,1)S(1)} %get-tuple-element.42, ...), kind=kLoop, calls=%fused_computation.145 | loop fusion | flops 14848 | bytes 19044 | tf_op jit(solution)/shard_map/sub | solution.py:50
  46.8 28.5 %all-to-all-done = bf16[32,32,896]{2,0,1:T(8,128)(2,1)S(1)} async-done(((bf16[32,32,896]{2,0,1:T(8,128)(2,1)}), bf16[32,32,896]{2,0,1:T(8,128)(2,1)S(1)}, u32[]{:S(2)}, u32[]{:S(2)}) %all-to-all-start) | async-done | bytes 1835040 | tf_op jit(solution)/shard_map/all_to_all | solution.py:60
  75.4 41.5 %all-gather.3.cloned.1.call-done = bf16[1024,3584]{1,0:T(8,128)(2,1)} async-done(((bf16[32,3584]{1,0:T(8,128)(2,1)}), bf16[1024,3584]{1,0:T(8,128)(2,1)}) %all-gather.3.cloned.1.call-update) | async-done | bytes 7340048 | tf_op jit(solution)/shard_map/all_gather | solution.py:61
  116.9 13.7 %convolution_convert_fusion.1 = bf16[512,896]{1,0:T(8,128)(2,1)} fusion(bf16[3584,896]{1,0:T(8,128)(2,1)} %param.8, bf16[1024,3584]{1,0:T(8,128)(2,1)} %all-gather.3.cloned.1.call-done, s32[512]{0:T(512)S(1)} %select_subtract_fusion), kind=kOutput, calls=%fused_computation.24 | convolution fusion | flops 7049248768 | bytes 14682112 | tf_op jit(solution)/shard_map/dot_general | solution.py:68
  130.5 18.9 %all_to_all.44 = bf16[8,64,896]{2,1,0:T(8,128)(2,1)S(1)} all-to-all(bf16[8,64,896]{2,1,0:T(8,128)(2,1)} %bitcast.134), channel_id=1, replica_groups=mesh['dp'=32,'tensor'=8] {'tensor'}, dimensions={0} | all-to-all | bytes 1835008 | tf_op jit(solution)/shard_map/all_to_all | solution.py:70
  149.6 17.7 %all_to_all.45 = bf16[8,64,896]{2,1,0:T(8,128)(2,1)} all-to-all(bf16[8,64,896]{2,1,0:T(8,128)(2,1)S(1)} %broadcast_in_dim.72), channel_id=1, replica_groups=mesh['dp'=32,'tensor'=8] {'tensor'}, dimensions={0} | all-to-all | bytes 1835008 | tf_op jit(solution)/shard_map/all_to_all | solution.py:28
  167.3 3.0 fusion.37
  170.3 33.0 %all_to_all.46 = f32[32,16,512]{2,1,0:T(8,128)S(1)} all-to-all(f32[32,16,512]{2,1,0:T(8,128)S(1)} %fusion.37), channel_id=1, replica_groups=mesh['dp'=32,'tensor'=8] {'dp'}, dimensions={0} | all-to-all | bytes 2097152 | tf_op jit(solution)/shard_map/all_to_all | solution.py:33
  204.5 7.5 %all-to-all-start.4 = ((f32[32,16,512]{2,1,0:T(8,128)}), f32[32,16,512]{2,1,0:T(8,128)S(1)}, u32[]{:S(2)}, u32[]{:S(2)}) async-start(f32[32,16,512]{2,1,0:T(8,128)} %broadcast_in_dim.73), calls=%async_computation.4 | async-start | bytes 2097152 | tf_op jit(solution)/shard_map/all_to_all | solution.py:28
  214.9 1.8 compare_and_fusion
  216.7 6.3 %fusion.88 = f32[1024,1024]{1,0:T(8,128)} fusion(bf16[1024,896]{1,0:T(8,128)(2,1)} %bitcast.131, bf16[1024,896]{1,0:T(8,128)(2,1)} %param.11), kind=kOutput, calls=%fused_computation.176 | convolution fusion | flops 1879048192 | bytes 7864320 | tf_op jit(solution)/shard_map/dot_general | solution.py:16
  223.0 15.5 %all-to-all-done.4 = f32[32,16,512]{2,1,0:T(8,128)S(1)} async-done(((f32[32,16,512]{2,1,0:T(8,128)}), f32[32,16,512]{2,1,0:T(8,128)S(1)}, u32[]{:S(2)}, u32[]{:S(2)}) %all-to-all-start.4) | async-done | bytes 1048608 | tf_op jit(solution)/shard_map/all_to_all | solution.py:28
  239.5 11.7 %cholesky.104 = f32[128,128]{1,0:T(8,128)S(1)} custom-call(f32[128,128]{1,0:T(8,128)S(1)} %cholesky.266), custom_call_target="Cholesky" | custom-call | tf_op jit(solution)/shard_map/jit(cholesky)/cholesky | solution.py:82
  251.4 9.8 %custom-call.32 = f32[1,128,128]{1,2,0:T(8,128)S(1)} custom-call(f32[1,128,128]{2,1,0:T(8,128)S(1)} %get-tuple-element.68), custom_call_target="InvertDiagBlocksLowerTriangular" | custom-call | tf_op jit(solution)/shard_map/jit(cholesky)/cholesky | solution.py:82
  261.9 12.1 %cholesky.217 = f32[128,128]{1,0:T(8,128)S(1)} custom-call(f32[128,128]{1,0:T(8,128)S(1)} %cholesky.270), custom_call_target="Cholesky" | custom-call | tf_op jit(solution)/shard_map/jit(cholesky)/cholesky | solution.py:82
  274.0 7.7 %all-to-all-start.5 = ((f32[32,32,1024]{2,1,0:T(8,128)}), f32[32,32,1024]{2,1,0:T(8,128)}, u32[]{:S(2)}, u32[]{:S(2)}) async-start(f32[32,32,1024]{2,1,0:T(8,128)} %bitcast.128), calls=%async_computation.5 | async-start | bytes 8388608 | tf_op jit(solution)/shard_map/all_to_all | solution.py:33
  281.7 9.8 %custom-call.33 = f32[1,128,128]{1,2,0:T(8,128)S(1)} custom-call(f32[1,128,128]{2,1,0:T(8,128)S(1)} %get-tuple-element.65), custom_call_target="InvertDiagBlocksLowerTriangular" | custom-call | tf_op jit(solution)/shard_map/jit(cholesky)/cholesky | solution.py:82
  292.2 11.7 %cholesky.238 = f32[128,128]{1,0:T(8,128)S(1)} custom-call(f32[128,128]{1,0:T(8,128)S(1)} %cholesky.275), custom_call_target="Cholesky" | custom-call | tf_op jit(solution)/shard_map/jit(cholesky)/cholesky | solution.py:82
  303.9 9.8 %custom-call.34 = f32[1,128,128]{1,2,0:T(8,128)S(1)} custom-call(f32[1,128,128]{2,1,0:T(8,128)S(1)} %get-tuple-element.62), custom_call_target="InvertDiagBlocksLowerTriangular" | custom-call | tf_op jit(solution)/shard_map/jit(cholesky)/cholesky | solution.py:82
  314.3 11.9 %cholesky.255 = f32[128,128]{1,0:T(8,128)S(1)} custom-call(f32[128,128]{1,0:T(8,128)S(1)} %convolution_subtract_fusion.6), custom_call_target="Cholesky" | custom-call | tf_op jit(solution)/shard_map/jit(cholesky)/cholesky | solution.py:82
  331.5 10.4 %while.1 = (s32[]{:T(128)}, f32[512,512]{1,0:T(8,128)S(1)}, s32[4,2]{0,1:T(2,128)S(1)}, f32[4,128,128]{2,1,0:T(8,128)}, s32[]{:T(128)}) while((s32[]{:T(128)}, f32[512,512]{1,0:T(8,128)S(1)}, s32[4,2]{0,1:T(2,128)S(1)}, f32[4,128,128]{2,1,0:T(8,128)}, s32[]{:T(128)}) %tuple.97), condition=%wide.while_cond, body=%wide.while_body.sunk | while | flops 2 | bytes 132705 | solution.py:86
  332.1 2.0 bitcast_dynamic-update-slice_fusion.2
  334.7 2.0 bitcast_dynamic-update-slice_fusion.2
  337.3 2.0 bitcast_dynamic-update-slice_fusion.2
  339.9 2.0 bitcast_dynamic-update-slice_fusion.2
  341.9 40.1 %custom-call.35 = f32[4,128,128]{1,2,0:T(8,128)S(1)} custom-call(f32[4,128,128]{2,1,0:T(8,128)} %get-tuple-element.21), custom_call_target="InvertDiagBlocksLowerTriangular" | custom-call | tf_op jit(solution)/shard_map/triangular_solve | solution.py:86
  382.7 2.9 fusion.84
  395.3 2.6 add_convert_fusion
  397.9 2.4 reduce_sum.42
  (96 shorter events, 29.8 us)
Async XLA Ops:
  7.2 109.7 %all-gather.3.cloned.1.call-start = ((), (), s32[]{:S(2)}) async-start(), calls=%async_computation.6 | async-start | bytes 7569408 | tf_op jit(solution)/shard_map/all_gather | solution.py:61
  9.0 203.3 %copy-start.4 = (pred[32]{0:T(512)(128)(4,1)}, pred[32]{0:T(512)(128)(4,1)S(1)}, u32[]{:S(2)}) copy-start(pred[32]{0:T(512)(128)(4,1)S(1)} %iota_compare_fusion.19) | copy-start | bytes 100
  12.9 11.8 %copy-start.6 = (s32[32]{0:T(128)S(1)}, s32[32]{0:T(128)}, u32[]{:S(2)}) copy-start(s32[32]{0:T(128)} %param.6) | copy-start | bytes 388
  12.9 62.5 %all-to-all-start = ((bf16[32,32,896]{2,0,1:T(8,128)(2,1)}), bf16[32,32,896]{2,0,1:T(8,128)(2,1)S(1)}, u32[]{:S(2)}, u32[]{:S(2)}) async-start(bf16[32,32,896]{2,0,1:T(8,128)(2,1)} %bitcast.127), calls=%async_computation | async-start | bytes 3670016 | tf_op jit(solution)/shard_map/all_to_all | solution.py:60
  75.4 91.9 %copy-start = (bf16[32,32,896]{2,0,1:T(8,128)(2,1)}, bf16[32,32,896]{2,0,1:T(8,128)(2,1)S(1)}, u32[]{:S(2)}) copy-start(bf16[32,32,896]{2,0,1:T(8,128)(2,1)S(1)} %all-to-all-done) | copy-start | bytes 5505028
  203.3 9.0 %copy-start.2 = (bf16[32,1024]{1,0:T(8,128)(2,1)S(1)}, bf16[32,1024]{1,0:T(8,128)(2,1)}, u32[]{:S(2)}) copy-start(bf16[32,1024]{1,0:T(8,128)(2,1)} %param.10) | copy-start | bytes 196612
  203.4 9.0 %copy-start.3 = (bf16[32,1024]{1,0:T(8,128)(2,1)S(1)}, bf16[32,1024]{1,0:T(8,128)(2,1)}, u32[]{:S(2)}) copy-start(bf16[32,1024]{1,0:T(8,128)(2,1)} %param.9) | copy-start | bytes 196612
  204.5 33.9 %all-to-all-start.4 = ((f32[32,16,512]{2,1,0:T(8,128)}), f32[32,16,512]{2,1,0:T(8,128)S(1)}, u32[]{:S(2)}, u32[]{:S(2)}) async-start(f32[32,16,512]{2,1,0:T(8,128)} %broadcast_in_dim.73), calls=%async_computation.4 | async-start | bytes 2097152 | tf_op jit(solution)/shard_map/all_to_all | solution.py:28
  212.1 119.0 %all-gather.5.cloned.1.call-start = ((), (), s32[]{:S(2)}) async-start(), calls=%async_computation.7 | async-start | bytes 2162688 | tf_op jit(solution)/shard_map/all_gather | solution.py:65
  274.0 123.9 %all-to-all-start.5 = ((f32[32,32,1024]{2,1,0:T(8,128)}), f32[32,32,1024]{2,1,0:T(8,128)}, u32[]{:S(2)}, u32[]{:S(2)}) async-start(f32[32,32,1024]{2,1,0:T(8,128)} %bitcast.128), calls=%async_computation.5 | async-start | bytes 8388608 | tf_op jit(solution)/shard_map/all_to_all | solution.py:33
  330.9 0.7 copy-start.9
  393.5 1.7 copy-start.1
  393.5 1.8 copy-start.7
  397.8 2.4 copy-start.5
  397.8 2.5 copy-start.8
Sparse Core Ops, SparseCore 0:
  11.6 105.2 all-gather.2
  216.1 81.9 all-gather.4
